TPU v7x, 256 devices: a whole 4x4x8 slice. The times are simulated.
256 devices in a mesh: expert: 32 (over z, y_hi, core), dp: 8 (over x, y_lo).
Axes of the slice: x: 4, y: 4 (y_hi: 2, y_lo: 2; y = y_hi * 2 + y_lo), z: 8, core: 2. Of those that a mesh axis runs over, the one named last changes fastest.
Arguments:
- tokens: bfloat16 [32768, 2048], P(('expert', 'dp')), may hold values from -6 to 6
- targets: bfloat16 [32768, 2048], P(('expert', 'dp')), may hold values from -6 to 6
- router: bfloat16 [2048, 32], replicated, may hold values from -0.125 to 0.125
- picks: int32 [32768, 32, 4], P(('expert', 'dp')), may hold values from 0 to 1, as said below
- w_gate_up: bfloat16 [32, 2, 1408, 2048], P('expert', None, 'dp'), may hold values from -0.125 to 0.125
- w_down: bfloat16 [32, 1408, 2048], P('expert', 'dp'), may hold values from -0.15625 to 0.15625
- v_gate_up: bfloat16 [32, 2, 1408, 2048], P('expert', None, 'dp'), may hold values from -0.125 to 0.125
- v_down: bfloat16 [32, 1408, 2048], P('expert', 'dp'), may hold values from -0.15625 to 0.15625
Outputs:
- mixed: bfloat16 [32768, 2048], P(('expert', 'dp'))
- hvp_gate_up: float32 [32, 2, 1408, 2048], P('expert', None, 'dp')
- hvp_down: float32 [32, 1408, 2048], P('expert', 'dp')
Inputs may be any that keep to these rules, and one draw needn't show every extreme that they name: In every block of 128 tokens (one device's rows), for each expert e and slot c exactly one token t has picks[t, e, c] = 1, and an expert never picks a token twice.
All inputs are finite; a program needn't handle non-finite values.
Results may differ from a plain program's by a relative error of at most 0.009.
Values may be sent and summed in bfloat16 or wider, within the bound.
No kernel may reach another device: no remote copies, remote signals or barrier semaphores. Data moves between devices by JAX's collectives and lax.ppermute only.
A program may use at most 128 MiB of HBM per device.

v0:
```python
import math

import jax
import jax.numpy as jnp
from jax import lax
from jax.sharding import PartitionSpec as P


def regroup(block, lead):
    count, total, width = block.shape
    parted = block.reshape(count, lead, total // lead, width)
    return jnp.swapaxes(parted, 0, 1).reshape(lead, count * total // lead, width)


def local(tokens, targets, router, picks, w_gate_up, w_down, v_gate_up, v_down):
    highest = lax.Precision.HIGHEST
    n_exp = lax.axis_size("expert")
    exp_dev = w_down.shape[0]
    onehot = picks.astype(jnp.bfloat16)
    gates = jax.nn.sigmoid(jnp.dot(tokens, router, preferred_element_type=jnp.float32))
    outgoing = jnp.einsum("tec,td->ecd", onehot, tokens, preferred_element_type=jnp.float32).astype(
        jnp.bfloat16
    )
    arrived = lax.all_to_all(outgoing, "expert", split_axis=0, concat_axis=0, tiled=True)
    rows = lax.all_gather(regroup(arrived, exp_dev), "dp", axis=1, tiled=True)
    scale = 1.0 / math.sqrt(rows.shape[1])
    primal = jnp.einsum("ekfd,erd->ekfr", w_gate_up, rows, preferred_element_type=jnp.float32)
    tangent = jnp.einsum("ekfd,erd->ekfr", v_gate_up, rows, preferred_element_type=jnp.float32)
    gate_pre, up_pre = (primal[:, 0], primal[:, 1])
    gate_dot, up_dot = (tangent[:, 0], tangent[:, 1])
    sigma = jax.nn.sigmoid(gate_pre)
    active = gate_pre * sigma
    slope = sigma * (1.0 + gate_pre * (1.0 - sigma))
    curve = sigma * (1.0 - sigma) * (2.0 + gate_pre * (1.0 - 2.0 * sigma))
    act_dot = slope * gate_dot
    hidden = (active * up_pre).astype(jnp.bfloat16)
    hidden_dot = (act_dot * up_pre + active * up_dot).astype(jnp.bfloat16)
    part_out = jnp.einsum("efr,efd->erd", hidden, w_down, preferred_element_type=jnp.float32)
    part_dot = jnp.einsum(
        "efr,efd->erd", hidden_dot, w_down, preferred_element_type=jnp.float32
    ) + jnp.einsum("efr,efd->erd", hidden, v_down, preferred_element_type=jnp.float32)
    own_out, own_dot = (
        lax.psum_scatter(part_out, "dp", scatter_dimension=1, tiled=True),
        lax.psum_scatter(part_dot, "dp", scatter_dimension=1, tiled=True),
    )
    back_out = regroup(own_out.astype(jnp.bfloat16), n_exp)
    back_dot = regroup(own_dot.astype(jnp.bfloat16), n_exp)
    ret_out, ret_dot = (
        lax.all_to_all(back_out, "expert", split_axis=0, concat_axis=0, tiled=True),
        lax.all_to_all(back_dot, "expert", split_axis=0, concat_axis=0, tiled=True),
    )
    ret_out = ret_out.astype(jnp.float32)
    ret_dot = ret_dot.astype(jnp.float32)
    weighted = picks.astype(jnp.float32) * gates[:, :, None]
    combined = jnp.einsum("tec,ecd->td", weighted, ret_out, precision=highest)
    combined_dot = jnp.einsum("tec,ecd->td", weighted, ret_dot, precision=highest)
    mixed = combined.astype(jnp.bfloat16)
    resid = scale * (combined - targets.astype(jnp.float32))
    resid_dot = scale * combined_dot
    cot_send = jnp.einsum("tec,td->ecd", weighted, resid, precision=highest).astype(jnp.bfloat16)
    cdot_send = jnp.einsum("tec,td->ecd", weighted, resid_dot, precision=highest).astype(
        jnp.bfloat16
    )
    cot_got, cdot_got = (
        lax.all_to_all(cot_send, "expert", split_axis=0, concat_axis=0, tiled=True),
        lax.all_to_all(cdot_send, "expert", split_axis=0, concat_axis=0, tiled=True),
    )
    own_cot = regroup(cot_got, exp_dev)
    own_cdot = regroup(cdot_got, exp_dev)
    cot_rows, cdot_rows = (
        lax.all_gather(own_cot, "dp", axis=1, tiled=True),
        lax.all_gather(own_cdot, "dp", axis=1, tiled=True),
    )
    grad_hid = jnp.einsum("erd,efd->efr", cot_rows, w_down, preferred_element_type=jnp.float32)
    grad_hdot = jnp.einsum(
        "erd,efd->efr", cdot_rows, w_down, preferred_element_type=jnp.float32
    ) + jnp.einsum("erd,efd->efr", cot_rows, v_down, preferred_element_type=jnp.float32)
    hvp_down = jnp.einsum(
        "efr,erd->efd", hidden_dot, cot_rows, preferred_element_type=jnp.float32
    ) + jnp.einsum("efr,erd->efd", hidden, cdot_rows, preferred_element_type=jnp.float32)
    gate_term = (
        (grad_hdot * up_pre + grad_hid * up_dot) * slope + grad_hid * up_pre * curve * gate_dot
    ).astype(jnp.bfloat16)
    up_term = (grad_hdot * active + grad_hid * act_dot).astype(jnp.bfloat16)
    both_terms = jnp.stack([gate_term, up_term], axis=1)
    hvp_gate_up = jnp.einsum("ekfr,erd->ekfd", both_terms, rows, preferred_element_type=jnp.float32)
    return (mixed, hvp_gate_up, hvp_down)


def solution(mesh):
    placed = (
        P(("expert", "dp"), None),
        P(("expert", "dp"), None),
        P(),
        P(("expert", "dp"), None, None),
        P("expert", None, "dp", None),
        P("expert", "dp", None),
        P("expert", None, "dp", None),
        P("expert", "dp", None),
    )
    return jax.shard_map(
        local,
        mesh=mesh,
        in_specs=placed,
        out_specs=(
            P(("expert", "dp"), None),
            P("expert", None, "dp", None),
            P("expert", "dp", None),
        ),
        check_vma=False,
    )
```

profile of v0, /device:TPU:56, one launch (start us, length us, event | category | flops | bytes accessed | tf_op | source)
XLA Modules:
  0.0 717.0 jit_solution(16694761618752664140)
XLA Ops:
  7.2 0.0 all-gather.4.cloned.1.call-start
  7.2 1.0 convert_element_type.62
  8.2 1.3 convolution_convert_fusion.2
  9.5 0.4 copy.35
  9.9 27.8 %all_to_all.25 = bf16[32,4,2048]{2,1,0:T(4,128)(2,1)S(1)} all-to-all(bf16[32,4,2048]{2,1,0:T(4,128)(2,1)S(1)} %copy.35), channel_id=1, replica_groups=mesh['expert'=32,'dp'=8] {'expert'}, dimensions={0} | all-to-all | bytes 1048576 | tf_op jit(solution)/shard_map/all_to_all | solution.py:24
  37.7 0.9 reshape_transpose_reshape.15
  38.7 0.0 reduce-scatter.3.cloned.1.call-start
  38.7 88.8 %all-gather.4.cloned.1.call-done = bf16[1,1024,2048]{2,1,0:T(8,128)(2,1)} async-done(((bf16[1,128,2048]{2,1,0:T(8,128)(2,1)}), bf16[1,1024,2048]{2,1,0:T(8,128)(2,1)}) %all-gather.4.cloned.1.call-update) | async-done | bytes 4194320 | tf_op jit(solution)/shard_map/all_gather | solution.py:25
  127.5 4.0 fusion.30
  131.6 1.8 fusion.27
  133.4 0.4 add_convert_fusion
  133.8 0.7 copy-done.9
  134.5 4.5 convolution_bitcast_fusion
  139.1 0.0 reduce-scatter.5.cloned.1.call-start
  139.1 1.3 fusion.74
  140.4 4.6 add_bitcast_fusion
  145.1 168.4 %reduce-scatter.3.cloned.1.call-done = f32[1,128,2048]{2,1,0:T(8,128)} async-done(((f32[1,1024,2048]{2,1,0:T(8,128)}), f32[1,128,2048]{2,1,0:T(8,128)}) %reduce-scatter.3.cloned.1.call-update) | async-done | bytes 1048592 | tf_op jit(solution)/shard_map/reduce_scatter | solution.py:43
  313.4 1.3 convert_element_type.66
  314.7 1.0 reshape_transpose_reshape.16
  315.7 10.0 %all-to-all-start.1 = ((bf16[32,4,2048]{2,1,0:T(4,128)(2,1)}), bf16[32,4,2048]{2,1,0:T(4,128)(2,1)S(1)}, u32[]{:S(2)}, u32[]{:S(2)}) async-start(bf16[32,4,2048]{2,1,0:T(4,128)(2,1)} %reshape_transpose_reshape.16), calls=%async_computation.2 | async-start | bytes 1048576 | tf_op jit(solution)/shard_map/all_to_all | solution.py:49
  325.8 0.0 all-gather.8.cloned.1.call-start
  325.8 0.3 fusion.46
  326.2 16.4 %all-to-all-done.1 = bf16[32,4,2048]{2,1,0:T(4,128)(2,1)S(1)} async-done(((bf16[32,4,2048]{2,1,0:T(4,128)(2,1)}), bf16[32,4,2048]{2,1,0:T(4,128)(2,1)S(1)}, u32[]{:S(2)}, u32[]{:S(2)}) %all-to-all-start.1) | async-done | bytes 524320 | tf_op jit(solution)/shard_map/all_to_all | solution.py:49
  342.6 1.6 fusion.94
  344.2 1.1 convolution_convert_fusion
  345.3 0.4 copy.43
  345.7 23.6 %all_to_all.26 = bf16[32,4,2048]{2,1,0:T(4,128)(2,1)S(1)} all-to-all(bf16[32,4,2048]{2,1,0:T(4,128)(2,1)S(1)} %copy.43), channel_id=1, replica_groups=mesh['expert'=32,'dp'=8] {'expert'}, dimensions={0} | all-to-all | bytes 1048576 | tf_op jit(solution)/shard_map/all_to_all | solution.py:65
  369.3 0.9 reshape_transpose_reshape.19
  370.2 0.0 all-gather.6.cloned.1.call-start
  370.2 128.9 %reduce-scatter.5.cloned.1.call-done = f32[1,128,2048]{2,1,0:T(8,128)} async-done(((f32[1,1024,2048]{2,1,0:T(8,128)}), f32[1,128,2048]{2,1,0:T(8,128)}) %reduce-scatter.5.cloned.1.call-update) | async-done | bytes 1048592 | tf_op jit(solution)/shard_map/reduce_scatter | solution.py:44
  499.1 1.3 convert_element_type.70
  500.4 0.2 reshape_transpose_reshape.17
  500.6 25.9 %all_to_all.27 = bf16[32,4,2048]{2,1,0:T(4,128)(2,1)S(1)} all-to-all(bf16[32,4,2048]{2,1,0:T(4,128)(2,1)S(1)} %reshape_transpose_reshape.17), channel_id=1, replica_groups=mesh['expert'=32,'dp'=8] {'expert'}, dimensions={0} | all-to-all | bytes 1048576 | tf_op jit(solution)/shard_map/all_to_all | solution.py:50
  526.5 0.8 fusion.26
  527.3 1.0 convolution_convert_fusion.1
  528.3 0.4 copy.41
  528.7 23.7 %all_to_all.28 = bf16[32,4,2048]{2,1,0:T(4,128)(2,1)S(1)} all-to-all(bf16[32,4,2048]{2,1,0:T(4,128)(2,1)S(1)} %copy.41), channel_id=1, replica_groups=mesh['expert'=32,'dp'=8] {'expert'}, dimensions={0} | all-to-all | bytes 1048576 | tf_op jit(solution)/shard_map/all_to_all | solution.py:66
  552.4 0.9 reshape_transpose_reshape.18
  553.4 50.4 %all-gather.8.cloned.1.call-done = bf16[1,1024,2048]{2,1,0:T(8,128)(2,1)} async-done(((bf16[1,128,2048]{2,1,0:T(8,128)(2,1)}), bf16[1,1024,2048]{2,1,0:T(8,128)(2,1)}) %all-gather.8.cloned.1.call-update) | async-done | bytes 4194320 | tf_op jit(solution)/shard_map/all_gather | solution.py:71
  603.8 3.2 fusion
  607.0 0.2 copy-done.3
  607.2 2.4 fusion.35
  609.6 2.4 fusion.4
  612.1 87.1 %all-gather.6.cloned.1.call-done = bf16[1,1024,2048]{2,1,0:T(8,128)(2,1)} async-done(((bf16[1,128,2048]{2,1,0:T(8,128)(2,1)}), bf16[1,1024,2048]{2,1,0:T(8,128)(2,1)}) %all-gather.6.cloned.1.call-update) | async-done | bytes 4194320 | tf_op jit(solution)/shard_map/all_gather | solution.py:72
  699.2 4.4 fusion.22
  703.6 0.1 copy-done.10
  703.7 3.5 fusion.86
  707.3 3.3 fusion.16
  (41 shorter events, 0.2 us)
Async XLA Ops:
  7.2 120.4 %copy-start = (bf16[1,2,176,2048]{3,2,1,0:T(8,128)(2,1)S(1)}, bf16[1,2,176,2048]{3,2,1,0:T(8,128)(2,1)}, u32[]{:S(2)}) copy-start(bf16[1,2,176,2048]{3,2,1,0:T(8,128)(2,1)} %param.14) | copy-start | bytes 4325380
  7.2 120.3 %all-gather.4.cloned.1.call-start = ((), (), s32[]{:S(2)}) async-start(), calls=%async_computation.7 | async-start | bytes 4718592 | tf_op jit(solution)/shard_map/all_gather | solution.py:25
  38.6 92.9 %copy-start.18 = (bf16[1,2,176,2048]{3,2,1,0:T(8,128)(2,1)S(1)}, bf16[1,2,176,2048]{3,2,1,0:T(8,128)(2,1)}, u32[]{:S(2)}) copy-start(bf16[1,2,176,2048]{3,2,1,0:T(8,128)(2,1)} %param.12) | copy-start | bytes 4325380
  38.7 274.8 %reduce-scatter.3.cloned.1.call-start = ((), (), s32[]{:S(2)}) async-start(), calls=%async_computation.8 | async-start | bytes 9437184 | tf_op jit(solution)/shard_map/reduce_scatter | solution.py:43
  127.5 4.0 copy-start.16
  131.6 1.8 copy-start.7
  131.6 2.9 copy-start.4
  133.4 1.1 copy-start.9
  139.1 360.0 %reduce-scatter.5.cloned.1.call-start = ((), (), s32[]{:S(2)}) async-start(), calls=%async_computation.9 | async-start | bytes 9437184 | tf_op jit(solution)/shard_map/reduce_scatter | solution.py:44
  139.1 1.3 copy-start.11
  145.0 180.8 %copy-start.6 = (bf16[128,2048]{1,0:T(8,128)(2,1)S(1)}, bf16[128,2048]{1,0:T(8,128)(2,1)}, u32[]{:S(2)}) copy-start(bf16[128,2048]{1,0:T(8,128)(2,1)} %param.8) | copy-start | bytes 1572868
  145.0 180.8 %copy-start.15 = (bf16[2048,32]{0,1:T(8,128)(2,1)S(1)}, bf16[2048,32]{0,1:T(8,128)(2,1)}, u32[]{:S(2)}) copy-start(bf16[2048,32]{0,1:T(8,128)(2,1)} %param.10) | copy-start | bytes 393220
  145.0 181.1 %copy-start.14 = (s32[128,32,4]{0,2,1:T(4,128)S(1)}, s32[128,32,4]{0,2,1:T(4,128)}, u32[]{:S(2)}) copy-start(s32[128,32,4]{0,2,1:T(4,128)} %param.11) | copy-start | bytes 196612
  145.0 199.1 %copy-start.13 = (bf16[128,2048]{1,0:T(8,128)(2,1)S(1)}, bf16[128,2048]{1,0:T(8,128)(2,1)}, u32[]{:S(2)}) copy-start(bf16[128,2048]{1,0:T(8,128)(2,1)} %param.9) | copy-start | bytes 1572868
  315.7 26.9 %all-to-all-start.1 = ((bf16[32,4,2048]{2,1,0:T(4,128)(2,1)}), bf16[32,4,2048]{2,1,0:T(4,128)(2,1)S(1)}, u32[]{:S(2)}, u32[]{:S(2)}) async-start(bf16[32,4,2048]{2,1,0:T(4,128)(2,1)} %reshape_transpose_reshape.16), calls=%async_computation.2 | async-start | bytes 1048576 | tf_op jit(solution)/shard_map/all_to_all | solution.py:49
  325.8 278.0 %all-gather.8.cloned.1.call-start = ((), (), s32[]{:S(2)}) async-start(), calls=%async_computation.11 | async-start | bytes 4718592 | tf_op jit(solution)/shard_map/all_gather | solution.py:71
  370.2 329.0 %all-gather.6.cloned.1.call-start = ((), (), s32[]{:S(2)}) async-start(), calls=%async_computation.10 | async-start | bytes 4718592 | tf_op jit(solution)/shard_map/all_gather | solution.py:72
  528.7 78.3 %copy-start.5 = (bf16[1,176,2048]{2,1,0:T(8,128)(2,1)S(1)}, bf16[1,176,2048]{2,1,0:T(8,128)(2,1)}, u32[]{:S(2)}) copy-start(bf16[1,176,2048]{2,1,0:T(8,128)(2,1)} %param.13) | copy-start | bytes 2162692
  603.8 3.4 copy-start.3
  607.2 2.4 copy-start.12
  699.2 4.4 copy-start.2
  699.2 4.4 copy-start.8
  699.2 4.5 copy-start.10
  703.7 3.6 copy-start.17
  707.2 3.3 copy-start.1
Sparse Core Ops, SparseCore 0:
  38.8 88.7 all-gather.3
  139.2 174.2 reduce-scatter.2
  316.0 183.0 reduce-scatter.4
  501.3 102.3 all-gather.7
  605.4 93.7 all-gather.5
where the time goes:
time: 720 us; the launch traced here: 717 us
  waiting for transfers between devices  540 us (75%)
  blocking collectives  101 us (14%)
  matrix products  41.5 us (6%)
  between operations  14.1 us (2%)
  starting transfers between devices  10.3 us (1%)
    reduce_scatter x1, waiting for transfers between devices, local(): lax.psum_scatter(part_out, 'dp', scatter_dimension=1, tiled=True)  168 us
    reduce_scatter x1, waiting for transfers between devices, local(): lax.psum_scatter(part_dot, 'dp', scatter_dimension=1, tiled=True)  129 us
    all_gather x1, waiting for transfers between devices, local(): rows = lax.all_gather(regroup(arrived, exp_dev), 'dp', axis=1, tiled=True)  88.8 us
    all_gather x1, waiting for transfers between devices, local(): lax.all_gather(own_cdot, 'dp', axis=1, tiled=True)  87.1 us
    all_gather x1, waiting for transfers between devices, local(): lax.all_gather(own_cot, 'dp', axis=1, tiled=True)  50.4 us
    all_to_all x1, blocking collectives, local(): lax.all_to_all(outgoing, 'expert', split_axis=0, concat_axis=0, tiled=True)  27.8 us
    all_to_all x1, blocking collectives, local(): lax.all_to_all(back_dot, 'expert', split_axis=0, concat_axis=0, tiled=True)  25.9 us
    all_to_all x1, blocking collectives, local(): lax.all_to_all(cdot_send, 'expert', split_axis=0, concat_axis=0, tiled=True)  23.7 us
  transfers between devices with their start and end apart: 6, of which 6 were waited for; matrix products, arithmetic and copies ran while one was open for 4% of the time, Pallas kernels for 0%

commit v1 on v0

--- a/solution.py
+++ b/solution.py
@@ -12,6 +12,22 @@
     return jnp.swapaxes(parted, 0, 1).reshape(lead, count * total // lead, width)
 
 
+def gather_dp(block):
+    n_dp = lax.axis_size("dp")
+    copies = jnp.broadcast_to(block[None], (n_dp,) + block.shape)
+    got = lax.all_to_all(copies, "dp", split_axis=0, concat_axis=0, tiled=True)
+    k, e, r, d = block.shape
+    return jnp.moveaxis(got, 0, 2).reshape(k, e, n_dp * r, d)
+
+
+def scatter_sum_dp(part):
+    n_dp = lax.axis_size("dp")
+    k, e, rows, d = part.shape
+    blocks = jnp.moveaxis(part.reshape(k, e, n_dp, rows // n_dp, d), 2, 0)
+    got = lax.all_to_all(blocks, "dp", split_axis=0, concat_axis=0, tiled=True)
+    return jnp.sum(got.astype(jnp.float32), axis=0)
+
+
 def local(tokens, targets, router, picks, w_gate_up, w_down, v_gate_up, v_down):
     highest = lax.Precision.HIGHEST
     n_exp = lax.axis_size("expert")
@@ -22,7 +38,7 @@
         jnp.bfloat16
     )
     arrived = lax.all_to_all(outgoing, "expert", split_axis=0, concat_axis=0, tiled=True)
-    rows = lax.all_gather(regroup(arrived, exp_dev), "dp", axis=1, tiled=True)
+    rows = gather_dp(regroup(arrived, exp_dev)[None])[0]
     scale = 1.0 / math.sqrt(rows.shape[1])
     primal = jnp.einsum("ekfd,erd->ekfr", w_gate_up, rows, preferred_element_type=jnp.float32)
     tangent = jnp.einsum("ekfd,erd->ekfr", v_gate_up, rows, preferred_element_type=jnp.float32)
@@ -39,16 +55,13 @@
     part_dot = jnp.einsum(
         "efr,efd->erd", hidden_dot, w_down, preferred_element_type=jnp.float32
     ) + jnp.einsum("efr,efd->erd", hidden, v_down, preferred_element_type=jnp.float32)
-    own_out, own_dot = (
-        lax.psum_scatter(part_out, "dp", scatter_dimension=1, tiled=True),
-        lax.psum_scatter(part_dot, "dp", scatter_dimension=1, tiled=True),
+    own_both = scatter_sum_dp(jnp.stack([part_out, part_dot]).astype(jnp.bfloat16))
+    back_both = jnp.stack(
+        [regroup(own_both[0].astype(jnp.bfloat16), n_exp), regroup(own_both[1].astype(jnp.bfloat16), n_exp)],
+        axis=1,
     )
-    back_out = regroup(own_out.astype(jnp.bfloat16), n_exp)
-    back_dot = regroup(own_dot.astype(jnp.bfloat16), n_exp)
-    ret_out, ret_dot = (
-        lax.all_to_all(back_out, "expert", split_axis=0, concat_axis=0, tiled=True),
-        lax.all_to_all(back_dot, "expert", split_axis=0, concat_axis=0, tiled=True),
-    )
+    ret_both = lax.all_to_all(back_both, "expert", split_axis=0, concat_axis=0, tiled=True)
+    ret_out, ret_dot = (ret_both[:, 0], ret_both[:, 1])
     ret_out = ret_out.astype(jnp.float32)
     ret_dot = ret_dot.astype(jnp.float32)
     weighted = picks.astype(jnp.float32) * gates[:, :, None]
@@ -61,16 +74,12 @@
     cdot_send = jnp.einsum("tec,td->ecd", weighted, resid_dot, precision=highest).astype(
         jnp.bfloat16
     )
-    cot_got, cdot_got = (
-        lax.all_to_all(cot_send, "expert", split_axis=0, concat_axis=0, tiled=True),
-        lax.all_to_all(cdot_send, "expert", split_axis=0, concat_axis=0, tiled=True),
+    both_got = lax.all_to_all(
+        jnp.stack([cot_send, cdot_send], axis=1), "expert", split_axis=0, concat_axis=0, tiled=True
     )
-    own_cot = regroup(cot_got, exp_dev)
-    own_cdot = regroup(cdot_got, exp_dev)
-    cot_rows, cdot_rows = (
-        lax.all_gather(own_cot, "dp", axis=1, tiled=True),
-        lax.all_gather(own_cdot, "dp", axis=1, tiled=True),
-    )
+    own_both = jnp.stack([regroup(both_got[:, 0], exp_dev), regroup(both_got[:, 1], exp_dev)])
+    both_rows = gather_dp(own_both)
+    cot_rows, cdot_rows = (both_rows[0], both_rows[1])
     grad_hid = jnp.einsum("erd,efd->efr", cot_rows, w_down, preferred_element_type=jnp.float32)
     grad_hdot = jnp.einsum(
         "erd,efd->efr", cdot_rows, w_down, preferred_element_type=jnp.float32

time: 720 us -> 416 us (0.58)
  waiting for transfers between devices: 540 us -> 27.7 us
  blocking collectives: 101 us -> 311 us
  local copies, waits for them, and re-layouts: 6.23 us -> 24.7 us
  matrix products: 41.5 us -> 26.9 us
  between operations: 14.1 us -> 0.96 us
  other arithmetic: 3.98 us -> 16.2 us
    reduce_scatter x2 -> x0, waiting for transfers between devices: 297 us -> none  [the longest x1 168 us: local(): lax.psum_scatter(part_out, 'dp', scatter_dimension=1, tiled=True)]
    all_gather x3 -> x0, waiting for transfers between devices: 226 us -> none  [the longest x1 88.8 us: local(): rows = lax.all_gather(regroup(arrived, exp_dev), 'dp', axis=1, tiled=True)]
    all_to_all x3 -> x4, blocking collectives: 73.2 us -> 283 us  [the longest x2 152 us: gather_dp(): got = lax.all_to_all(copies, 'dp', split_axis=0, concat_axis=0, tiled=True)]
    all_to_all x1, waiting for transfers between devices: 16.4 us -> 27.7 us  [local(): lax.all_to_all(back_both, 'expert', split_axis=0, concat_axis=0, tiled=True)]
    transpose x0 -> x1, local copies, waits for them, and re-layouts: none -> 8.26 us  [scatter_sum_dp(): blocks = jnp.moveaxis(part.reshape(k, e, n_dp, rows // n_dp, d), 2, 0)]
  transfers between devices with their start and end apart: 6 -> 1, of which waited for: 6 -> 1; matrix products, arithmetic and copies ran while one was open for 4% -> 0% of each run, Pallas kernels for 0% -> 0%
where the time goes in v1:
time: 416 us
  blocking collectives  311 us (75%)
  waiting for transfers between devices  27.7 us (7%)
  matrix products  26.9 us (6%)
  local copies, waits for them, and re-layouts  24.7 us (6%)
  other arithmetic  16.2 us (4%)
  starting transfers between devices  7.99 us (2%)
    all_to_all x2, blocking collectives, gather_dp(): got = lax.all_to_all(copies, 'dp', split_axis=0, concat_axis=0, tiled=True)  152 us
    all_to_all x1, blocking collectives, scatter_sum_dp(): got = lax.all_to_all(blocks, 'dp', split_axis=0, concat_axis=0, tiled=True)  98 us
    all_to_all x1, blocking collectives, local(): lax.all_to_all(jnp.stack([cot_send, cdot_send], axis=1), 'expert', split_...  33.7 us
    all_to_all x1, blocking collectives, local(): lax.all_to_all(outgoing, 'expert', split_axis=0, concat_axis=0, tiled=True)  27.8 us
    all_to_all x1, waiting for transfers between devices, local(): lax.all_to_all(back_both, 'expert', split_axis=0, concat_axis=0, tiled=True)  27.7 us
  transfers between devices with their start and end apart: 1, of which 1 were waited for; matrix products, arithmetic and copies ran while one was open for 0% of the time, Pallas kernels for 0%

profile of v1, /device:TPU:56, one launch (start us, length us, event | category | flops | bytes accessed | tf_op | source)
XLA Modules:
  0.0 415.6 jit_solution(9745053373520766619)
XLA Ops:
  0.6 1.0 convert_element_type.95
  1.6 1.3 convolution_convert_fusion.2
  3.0 0.4 copy.27
  3.4 27.8 %all_to_all.30 = bf16[32,4,2048]{2,1,0:T(4,128)(2,1)S(1)} all-to-all(bf16[32,4,2048]{2,1,0:T(4,128)(2,1)S(1)} %copy.27), channel_id=1, replica_groups=mesh['expert'=32,'dp'=8] {'expert'}, dimensions={0} | all-to-all | bytes 1048576 | tf_op jit(solution)/shard_map/all_to_all | solution.py:40
  31.1 0.1 broadcast_in_dim.16
  31.3 0.5 broadcast_in_dim.17
  31.8 53.1 %all_to_all.31 = bf16[8,1,1,128,2048]{4,3,2,1,0:T(8,128)(2,1)S(1)} all-to-all(bf16[8,1,1,128,2048]{4,3,2,1,0:T(8,128)(2,1)S(1)} %broadcast_in_dim.17), channel_id=1, replica_groups=mesh['expert'=32,'dp'=8] {'dp'}, dimensions={0} | all-to-all | bytes 8388608 | tf_op jit(solution)/shard_map/all_to_all | solution.py:18
  84.9 1.8 convolution_bitcast_fusion.3
  86.7 0.2 copy-done.2
  86.8 0.5 copy-done.16
  87.3 1.7 convolution_bitcast_fusion.4
  89.0 0.4 multiply_convert_fusion
  89.4 1.3 convert_bitcast_fusion
  90.8 1.3 fusion.39
  92.1 3.3 add_convert_fusion
  95.4 6.2 %maximum_bitcast_fusion = bf16[8,2,1,128,2048]{4,3,0,2,1:T(8,128)(2,1)} fusion(bf16[1,1,8,128,2048]{4,3,2,1,0:T(8,128)(2,1)} %bitcast.190, bf16[1,1,8,128,2048]{4,3,2,1,0:T(8,128)(2,1)S(1)} %convert_bitcast_fusion), kind=kLoop, calls=%fused_computation | loop fusion | flops 4194304 | bytes 16777216 | tf_op jit(solution)/shard_map/transpose | solution.py:26
  101.6 8.3 %copy.29 = bf16[8,2,1,128,2048]{4,3,2,1,0:T(8,128)(2,1)} copy(bf16[8,2,1,128,2048]{4,3,0,2,1:T(8,128)(2,1)} %maximum_bitcast_fusion) | data formatting | bytes 16777216 | tf_op jit(solution)/shard_map/transpose | solution.py:26
  109.8 98.0 %all_to_all.32 = bf16[8,2,1,128,2048]{4,3,2,1,0:T(8,128)(2,1)} all-to-all(bf16[8,2,1,128,2048]{4,3,2,1,0:T(8,128)(2,1)} %copy.29), channel_id=1, replica_groups=mesh['expert'=32,'dp'=8] {'dp'}, dimensions={0} | all-to-all | bytes 16777216 | tf_op jit(solution)/shard_map/all_to_all | solution.py:27
  207.8 5.2 %reduce.1 = bf16[2,128,2048]{2,1,0:T(8,128)(2,1)S(1)} reduce(bf16[8,2,1,128,2048]{4,3,2,1,0:T(8,128)(2,1)} %all_to_all.32, bf16[]{:T(256)} %constant.16), dimensions={0,2}, to_apply=%region_0.0.clone | reduce | flops 3670016 | bytes 9437186 | tf_op jit(solution)/shard_map/reduce_sum | solution.py:28
  213.0 1.1 fusion.64
  214.1 2.1 convert_element_type.102
  216.2 2.1 convert_element_type.103
  218.3 2.0 pad_maximum_fusion
  220.2 1.6 copy.30
  221.8 8.0 %all-to-all-start.3 = ((bf16[32,2,4,2048]{3,2,1,0:T(4,128)(2,1)}), bf16[32,2,4,2048]{3,2,1,0:T(4,128)(2,1)S(1)}, u32[]{:S(2)}, u32[]{:S(2)}) async-start(bf16[32,2,4,2048]{3,2,1,0:T(4,128)(2,1)} %copy.30), calls=%async_computation.3 | async-start | bytes 2097152 | tf_op jit(solution)/shard_map/all_to_all | solution.py:63
  229.8 0.3 fusion.10
  230.2 27.7 %all-to-all-done.3 = bf16[32,2,4,2048]{3,2,1,0:T(4,128)(2,1)S(1)} async-done(((bf16[32,2,4,2048]{3,2,1,0:T(4,128)(2,1)}), bf16[32,2,4,2048]{3,2,1,0:T(4,128)(2,1)S(1)}, u32[]{:S(2)}, u32[]{:S(2)}) %all-to-all-start.3) | async-done | bytes 1048608 | tf_op jit(solution)/shard_map/all_to_all | solution.py:63
  257.9 0.5 fusion.63
  258.4 0.8 fusion.2
  259.2 1.0 fusion.4
  260.2 1.6 fusion.65
  261.8 1.1 fusion.3
  263.0 0.8 copy.37
  263.8 33.7 %all_to_all.33 = bf16[32,2,4,2048]{3,2,1,0:T(4,128)(2,1)S(1)} all-to-all(bf16[32,2,4,2048]{3,2,1,0:T(4,128)(2,1)S(1)} %copy.37), channel_id=1, replica_groups=mesh['expert'=32,'dp'=8] {'expert'}, dimensions={0} | all-to-all | bytes 2097152 | tf_op jit(solution)/shard_map/all_to_all | solution.py:77
  297.5 1.3 fusion.62
  298.8 2.0 stack_reshape_transpose_reshape_squeeze.6
  300.8 0.9 stack_reshape_transpose_reshape_squeeze.7
  301.7 1.3 maximum_bitcast_fusion.1
  303.0 1.1 broadcast_in_dim.19
  304.0 98.7 %all_to_all.34 = bf16[8,2,1,128,2048]{4,3,2,1,0:T(8,128)(2,1)S(1)} all-to-all(bf16[8,2,1,128,2048]{4,3,2,1,0:T(8,128)(2,1)S(1)} %broadcast_in_dim.19), channel_id=1, replica_groups=mesh['expert'=32,'dp'=8] {'dp'}, dimensions={0} | all-to-all | bytes 16777216 | tf_op jit(solution)/shard_map/all_to_all | solution.py:18
  402.7 1.2 fusion.61
  403.9 1.5 convolution_bitcast_fusion.5
  405.5 1.0 fusion.47
  406.4 1.5 fusion.37
  408.0 2.1 fusion
  410.1 2.1 fusion.53
  412.2 0.1 copy-done.3
  412.3 3.3 convolution_bitcast_fusion
  (33 shorter events, 0.2 us)
Async XLA Ops:
  0.6 84.3 %copy-start = (bf16[1,2,176,2048]{3,2,1,0:T(8,128)(2,1)S(1)}, bf16[1,2,176,2048]{3,2,1,0:T(8,128)(2,1)}, u32[]{:S(2)}) copy-start(bf16[1,2,176,2048]{3,2,1,0:T(8,128)(2,1)} %param.14) | copy-start | bytes 4325380
  84.9 1.9 copy-start.2
  84.9 2.4 copy-start.16
  87.3 1.7 copy-start.7
  87.3 2.1 copy-start.4
  89.0 1.7 copy-start.9
  90.8 1.3 copy-start.11
  214.1 15.7 %copy-start.6 = (bf16[128,2048]{1,0:T(8,128)(2,1)S(1)}, bf16[128,2048]{1,0:T(8,128)(2,1)}, u32[]{:S(2)}) copy-start(bf16[128,2048]{1,0:T(8,128)(2,1)} %param.8) | copy-start | bytes 1572868
  214.1 15.7 %copy-start.15 = (bf16[2048,32]{0,1:T(8,128)(2,1)S(1)}, bf16[2048,32]{0,1:T(8,128)(2,1)}, u32[]{:S(2)}) copy-start(bf16[2048,32]{0,1:T(8,128)(2,1)} %param.10) | copy-start | bytes 393220
  216.2 13.9 %copy-start.14 = (s32[128,32,4]{0,2,1:T(4,128)S(1)}, s32[128,32,4]{0,2,1:T(4,128)}, u32[]{:S(2)}) copy-start(s32[128,32,4]{0,2,1:T(4,128)} %param.11) | copy-start | bytes 196612
  221.8 36.1 %all-to-all-start.3 = ((bf16[32,2,4,2048]{3,2,1,0:T(4,128)(2,1)}), bf16[32,2,4,2048]{3,2,1,0:T(4,128)(2,1)S(1)}, u32[]{:S(2)}, u32[]{:S(2)}) async-start(bf16[32,2,4,2048]{3,2,1,0:T(4,128)(2,1)} %copy.30), calls=%async_computation.3 | async-start | bytes 2097152 | tf_op jit(solution)/shard_map/all_to_all | solution.py:63
  230.1 31.7 %copy-start.13 = (bf16[128,2048]{1,0:T(8,128)(2,1)S(1)}, bf16[128,2048]{1,0:T(8,128)(2,1)}, u32[]{:S(2)}) copy-start(bf16[128,2048]{1,0:T(8,128)(2,1)} %param.9) | copy-start | bytes 1572868
  402.7 1.2 copy-start.5
  408.0 2.1 copy-start.8
  408.0 2.1 copy-start.10
  408.0 2.1 copy-start.12
  410.1 2.2 copy-start.3
  412.2 3.4 copy-start.1

commit v2 on v1

--- a/solution.py
+++ b/solution.py
@@ -12,20 +12,51 @@
     return jnp.swapaxes(parted, 0, 1).reshape(lead, count * total // lead, width)
 
 
+def _perms(n_dp):
+    nx = n_dp // 2
+    idx = lambda a, b: 2 * (a % nx) + b
+    partner = [(idx(a, b), idx(a, 1 - b)) for a in range(nx) for b in range(2)]
+    xplus = [(idx(a, b), idx(a + 1, b)) for a in range(nx) for b in range(2)]
+    xminus = [(idx(a, b), idx(a - 1, b)) for a in range(nx) for b in range(2)]
+    return partner, xplus, xminus
+
+
+def tree_gather(block):
+    partner, xplus, xminus = _perms(lax.axis_size("dp"))
+    send = lambda v, perm: lax.ppermute(v, "dp", perm)
+    half = block.shape[0] // 2
+    Pb = send(block, partner)
+    L = send(block, xplus)
+    R = send(block, xminus)
+    O = jnp.concatenate([send(L[:half], xplus), send(R[half:], xminus)])
+    PL = send(Pb, xplus)
+    PR = send(Pb, xminus)
+    Q = send(O, partner)
+    return jnp.stack([block, Pb, L, R, O, PL, PR, Q])
+
+
+def tree_scatter_sum(acc):
+    partner, xplus, xminus = _perms(lax.axis_size("dp"))
+    send = lambda v, perm: lax.ppermute(v.astype(jnp.bfloat16), "dp", perm).astype(jnp.float32)
+    half = acc.shape[1] // 2
+    a4 = acc[4] + send(acc[7], partner)
+    a2 = acc[2] + jnp.concatenate([send(a4[:half], xminus), jnp.zeros_like(a4[half:])])
+    a3 = acc[3] + jnp.concatenate([jnp.zeros_like(a4[:half]), send(a4[half:], xplus)])
+    a1 = acc[1] + send(acc[5], xminus) + send(acc[6], xplus)
+    return acc[0] + send(a1, partner) + send(a2, xminus) + send(a3, xplus)
+
+
 def gather_dp(block):
-    n_dp = lax.axis_size("dp")
-    copies = jnp.broadcast_to(block[None], (n_dp,) + block.shape)
-    got = lax.all_to_all(copies, "dp", split_axis=0, concat_axis=0, tiled=True)
     k, e, r, d = block.shape
-    return jnp.moveaxis(got, 0, 2).reshape(k, e, n_dp * r, d)
+    got = tree_gather(jnp.moveaxis(block, 2, 0))
+    return jnp.moveaxis(got.reshape(-1, k, e, d), 0, 2)
 
 
 def scatter_sum_dp(part):
     n_dp = lax.axis_size("dp")
     k, e, rows, d = part.shape
-    blocks = jnp.moveaxis(part.reshape(k, e, n_dp, rows // n_dp, d), 2, 0)
-    got = lax.all_to_all(blocks, "dp", split_axis=0, concat_axis=0, tiled=True)
-    return jnp.sum(got.astype(jnp.float32), axis=0)
+    blocks = jnp.moveaxis(part.astype(jnp.float32).reshape(k, e, n_dp, rows // n_dp, d), 2, 0)
+    return tree_scatter_sum(blocks)
 
 
 def local(tokens, targets, router, picks, w_gate_up, w_down, v_gate_up, v_down):
@@ -55,7 +86,7 @@
     part_dot = jnp.einsum(
         "efr,efd->erd", hidden_dot, w_down, preferred_element_type=jnp.float32
     ) + jnp.einsum("efr,efd->erd", hidden, v_down, preferred_element_type=jnp.float32)
-    own_both = scatter_sum_dp(jnp.stack([part_out, part_dot]).astype(jnp.bfloat16))
+    own_both = scatter_sum_dp(jnp.stack([part_out, part_dot]))
     back_both = jnp.stack(
         [regroup(own_both[0].astype(jnp.bfloat16), n_exp), regroup(own_both[1].astype(jnp.bfloat16), n_exp)],
         axis=1,

time: 416 us -> 326 us (0.78)
  the two profiles are of different devices: /device:TPU:56 before, /device:TPU:16 now
where the time goes in v2:
time: 326 us; the launch traced here: 320 us
  waiting for transfers between devices  138 us (42%)
  blocking collectives  62.8 us (19%)
  starting transfers between devices  45.2 us (14%)
  matrix products  30.6 us (9%)
  local copies, waits for them, and re-layouts  29.7 us (9%)
  other arithmetic  12.5 us (4%)
    ppermute x16, waiting for transfers between devices, tree_gather(): send = lambda v, perm: lax.ppermute(v, 'dp', perm)  64.1 us
    ppermute x8, waiting for transfers between devices, tree_scatter_sum(): lax.ppermute(v.astype(jnp.bfloat16), 'dp', perm).astype(jnp.float32)  45 us
    all_to_all x1, blocking collectives, local(): lax.all_to_all(jnp.stack([cot_send, cdot_send], axis=1), 'expert', split_...  33.7 us
    all_to_all x1, blocking collectives, local(): lax.all_to_all(outgoing, 'expert', split_axis=0, concat_axis=0, tiled=True)  29.1 us
    all_to_all x1, waiting for transfers between devices, local(): lax.all_to_all(back_both, 'expert', split_axis=0, concat_axis=0, tiled=True)  28.6 us
    ppermute x16, starting transfers between devices, tree_gather(): send = lambda v, perm: lax.ppermute(v, 'dp', perm)  25 us
    ppermute x8, starting transfers between devices, tree_scatter_sum(): lax.ppermute(v.astype(jnp.bfloat16), 'dp', perm).astype(jnp.float32)  12 us
    unnamed x49, local copies, waits for them, and re-layouts  9.72 us
  transfers between devices with their start and end apart: 25, of which 14 were waited for; matrix products, arithmetic and copies ran while one was open for 6% of the time, Pallas kernels for 0%

profile of v2, /device:TPU:16, one launch (start us, length us, event | category | flops | bytes accessed | tf_op | source)
XLA Modules:
  0.0 319.9 jit_solution(14376891591459352404)
XLA Ops:
  1.6 1.3 convolution_convert_fusion.2
  3.4 29.1 %all_to_all.15 = bf16[32,4,2048]{2,1,0:T(4,128)(2,1)S(1)} all-to-all(bf16[32,4,2048]{2,1,0:T(4,128)(2,1)S(1)} %copy.53), channel_id=1, replica_groups=mesh['expert'=32,'dp'=8] {'expert'}, dimensions={0} | all-to-all | bytes 1048576 | tf_op jit(solution)/shard_map/all_to_all | solution.py:71
  33.4 1.5 collective-permute-start.1
  34.9 1.7 collective-permute-start.2
  36.6 1.3 collective-permute-start
  38.1 9.8 %collective-permute-done.1 = bf16[128,1,1,2048]{3,0,2,1:T(8,128)(2,1)S(1)} collective-permute-done((bf16[128,1,1,2048]{3,0,2,1:T(8,128)(2,1)}, bf16[128,1,1,2048]{3,0,2,1:T(8,128)(2,1)S(1)}, u32[]{:S(2)}, u32[]{:S(2)}) %collective-permute-start.1) | collective-permute-done | bytes 524320 | tf_op jit(solution)/shard_map/ppermute | solution.py:26
  49.2 3.0 collective-permute-start.4
  52.3 3.2 %collective-permute-start.6 = (bf16[128,1,1,2048]{3,0,2,1:T(8,128)(2,1)}, bf16[128,1,1,2048]{3,0,2,1:T(8,128)(2,1)S(1)}, u32[]{:S(2)}, u32[]{:S(2)}) collective-permute-start(bf16[128,1,1,2048]{3,0,2,1:T(8,128)(2,1)} %collective-permute-done), channel_id=1, source_target_pairs={{0,6},{1,7},{2,0},{3,1},{4,2},{5,3},{6,4},{7,5},{8,14},{9,15},{10,... | collective-permute-start | bytes 1572872 | tf_op jit(solution)/shard_map/ppermute | solution.py:26
  59.0 1.5 collective-permute-start.7
  60.6 6.4 %collective-permute-done.5 = bf16[128,1,1,2048]{3,0,2,1:T(8,128)(2,1)S(1)} collective-permute-done((bf16[128,1,1,2048]{3,0,2,1:T(8,128)(2,1)}, bf16[128,1,1,2048]{3,0,2,1:T(8,128)(2,1)S(1)}, u32[]{:S(2)}, u32[]{:S(2)}) %collective-permute-start.5) | collective-permute-done | bytes 524320 | tf_op jit(solution)/shard_map/ppermute | solution.py:26
  67.5 1.7 collective-permute-done.7
  69.3 1.8 convolution_bitcast_fusion.4
  71.1 1.7 convolution_bitcast_fusion.5
  74.0 1.3 fusion.59
  75.3 1.3 convolution_bitcast_fusion
  76.6 1.3 convolution_add_fusion
  78.4 1.4 collective-permute-start.11
  79.7 2.9 collective-permute-start.8
  82.6 17.2 %collective-permute-done.11 = bf16[2,1,128,2048]{3,2,0,1:T(8,128)(2,1)S(1)} collective-permute-done((bf16[2,1,128,2048]{3,2,0,1:T(8,128)(2,1)S(1)}, bf16[2,1,128,2048]{3,2,0,1:T(8,128)(2,1)S(1)}, u32[]{:S(2)}, u32[]{:S(2)}) %collective-permute-start.11) | collective-permute-done | bytes 1048608 | tf_op jit(solution)/shard_map/ppermute | solution.py:40
  101.0 2.9 collective-permute-start.12
  103.9 2.0 maximum_bitcast_fusion
  106.2 6.2 %collective-permute-done.12 = bf16[1,1,128,2048]{3,2,0,1:T(8,128)(2,1)} collective-permute-done((bf16[1,1,128,2048]{3,2,0,1:T(8,128)(2,1)S(1)}, bf16[1,1,128,2048]{3,2,0,1:T(8,128)(2,1)}, u32[]{:S(2)}, u32[]{:S(2)}) %collective-permute-start.12) | collective-permute-done | bytes 524320 | tf_op jit(solution)/shard_map/ppermute | solution.py:40
  112.5 3.4 %fusion.19 = (bf16[2,1,128,2048]{3,2,0,1:T(8,128)(2,1)}, bf16[2,1,128,2048]{3,2,0,1:T(8,128)(2,1)}) fusion(bf16[2,1,128,2048]{3,2,0,1:T(8,128)(2,1)} %collective-permute-done.9, bf16[2,1,128,2048]{3,2,0,1:T(8,128)(2,1)S(1)} %collective-permute-done.8, bf16[1,1,128,2048]{3,2,0,1:T(8,128)(2,1)} %collective-permute-done.12, ...), kind=kLoop, calls=%fused_computation.34 | loop fusion | flops 8388608 | bytes 21495808 | tf_op jit(solution)/shard_map/convert_element_type | solution.py:40
  116.6 3.8 %collective-permute-start.13 = (bf16[2,1,128,2048]{3,2,0,1:T(8,128)(2,1)}, bf16[2,1,128,2048]{3,2,0,1:T(8,128)(2,1)S(1)}, u32[]{:S(2)}, u32[]{:S(2)}) collective-permute-start(bf16[2,1,128,2048]{3,2,0,1:T(8,128)(2,1)} %get-tuple-element.4), channel_id=1, source_target_pairs={{0,6},{1,7},{2,0},{3,1},{4,2},{5,3},{6,4},{7,5},{8,14},{9,15},{10,... | collective-permute-start | bytes 3145736 | tf_op jit(solution)/shard_map/ppermute | solution.py:40
  120.8 16.7 %collective-permute-done.10 = bf16[2,1,128,2048]{3,2,0,1:T(8,128)(2,1)S(1)} collective-permute-done((bf16[2,1,128,2048]{3,2,0,1:T(8,128)(2,1)}, bf16[2,1,128,2048]{3,2,0,1:T(8,128)(2,1)S(1)}, u32[]{:S(2)}, u32[]{:S(2)}) %collective-permute-start.10) | collective-permute-done | bytes 1048608 | tf_op jit(solution)/shard_map/ppermute | solution.py:40
  137.4 1.4 collective-permute-done.13
  138.9 3.4 %collective-permute-done.15 = bf16[2,1,128,2048]{3,2,0,1:T(8,128)(2,1)S(1)} collective-permute-done((bf16[2,1,128,2048]{3,2,0,1:T(8,128)(2,1)S(1)}, bf16[2,1,128,2048]{3,2,0,1:T(8,128)(2,1)S(1)}, u32[]{:S(2)}, u32[]{:S(2)}) %collective-permute-start.15) | collective-permute-done | bytes 1048608 | tf_op jit(solution)/shard_map/ppermute | solution.py:40
  143.9 1.2 convert_element_type.167
  146.1 2.7 pad_maximum_fusion
  148.8 8.2 %all-to-all-start.1 = ((bf16[32,2,4,2048]{3,2,1,0:T(4,128)(2,1)}), bf16[32,2,4,2048]{3,2,1,0:T(4,128)(2,1)S(1)}, u32[]{:S(2)}, u32[]{:S(2)}) async-start(bf16[32,2,4,2048]{3,2,1,0:T(4,128)(2,1)} %pad_maximum_fusion), calls=%async_computation.1 | async-start | bytes 2097152 | tf_op jit(solution)/shard_map/all_to_all | solution.py:94
  157.4 28.6 %all-to-all-done.1 = bf16[32,2,4,2048]{3,2,1,0:T(4,128)(2,1)S(1)} async-done(((bf16[32,2,4,2048]{3,2,1,0:T(4,128)(2,1)}), bf16[32,2,4,2048]{3,2,1,0:T(4,128)(2,1)S(1)}, u32[]{:S(2)}, u32[]{:S(2)}) %all-to-all-start.1) | async-done | bytes 1048608 | tf_op jit(solution)/shard_map/all_to_all | solution.py:94
  186.5 1.6 fusion.84
  189.9 2.1 fusion.9
  192.9 33.7 %all_to_all.16 = bf16[32,2,4,2048]{3,2,1,0:T(4,128)(2,1)S(1)} all-to-all(bf16[32,2,4,2048]{3,2,1,0:T(4,128)(2,1)S(1)} %copy.68), channel_id=1, replica_groups=mesh['expert'=32,'dp'=8] {'expert'}, dimensions={0} | all-to-all | bytes 2097152 | tf_op jit(solution)/shard_map/all_to_all | solution.py:108
  226.7 1.3 fusion.80
  229.8 3.2 %collective-permute-start.18 = (bf16[128,2,1,2048]{3,0,2,1:T(8,128)(2,1)S(1)}, bf16[128,2,1,2048]{3,0,2,1:T(8,128)(2,1)S(1)}, u32[]{:S(2)}, u32[]{:S(2)}) collective-permute-start(bf16[128,2,1,2048]{3,0,2,1:T(8,128)(2,1)S(1)} %bitcast.307), channel_id=1, source_target_pairs={{0,6},{1,7},{2,0},{3,1},{4,2},{5,3},{6,4},{7,5},{8,14},{9,15},{10,... | collective-permute-start | bytes 3145736 | tf_op jit(solution)/shard_map/ppermute | solution.py:26
  235.0 20.6 %collective-permute-done.17 = bf16[128,2,1,2048]{3,0,1,2:T(8,128)(2,1)S(1)} collective-permute-done((bf16[128,2,1,2048]{3,0,1,2:T(8,128)(2,1)S(1)}, bf16[128,2,1,2048]{3,0,1,2:T(8,128)(2,1)S(1)}, u32[]{:S(2)}, u32[]{:S(2)}) %collective-permute-start.17) | collective-permute-done | bytes 1048608 | tf_op jit(solution)/shard_map/ppermute | solution.py:26
  255.8 3.3 %collective-permute-start.20 = (bf16[64,2,1,2048]{3,0,2,1:T(8,128)(2,1)S(1)}, bf16[64,2,1,2048]{3,0,2,1:T(8,128)(2,1)S(1)}, u32[]{:S(2)}, u32[]{:S(2)}) collective-permute-start(bf16[64,2,1,2048]{3,0,2,1:T(8,128)(2,1)S(1)} %slice.134), channel_id=1, source_target_pairs={{0,6},{1,7},{2,0},{3,1},{4,2},{5,3},{6,4},{7,5},{8,14},{9,15},{10,... | collective-permute-start | bytes 1572872 | tf_op jit(solution)/shard_map/ppermute | solution.py:26
  259.1 3.2 %collective-permute-start.22 = (bf16[128,2,1,2048]{3,0,1,2:T(8,128)(2,1)S(1)}, bf16[128,2,1,2048]{3,0,1,2:T(8,128)(2,1)S(1)}, u32[]{:S(2)}, u32[]{:S(2)}) collective-permute-start(bf16[128,2,1,2048]{3,0,1,2:T(8,128)(2,1)S(1)} %collective-permute-done.16), channel_id=1, source_target_pairs={{0,6},{1,7},{2,0},{3,1},{4,2},{5,3},{6,4},{7,5},{8,14},{9,15},{10,... | collective-permute-start | bytes 3145736 | tf_op jit(solution)/shard_map/ppermute | solution.py:26
  265.4 6.3 %collective-permute-done.19 = bf16[64,2,1,2048]{3,0,1,2:T(8,128)(2,1)S(1)} collective-permute-done((bf16[64,2,1,2048]{3,0,1,2:T(8,128)(2,1)S(1)}, bf16[64,2,1,2048]{3,0,1,2:T(8,128)(2,1)S(1)}, u32[]{:S(2)}, u32[]{:S(2)}) %collective-permute-start.19) | collective-permute-done | bytes 524320 | tf_op jit(solution)/shard_map/ppermute | solution.py:26
  274.1 17.7 %collective-permute-done.21 = bf16[128,2,1,2048]{3,0,1,2:T(8,128)(2,1)S(1)} collective-permute-done((bf16[128,2,1,2048]{3,0,1,2:T(8,128)(2,1)S(1)}, bf16[128,2,1,2048]{3,0,1,2:T(8,128)(2,1)S(1)}, u32[]{:S(2)}, u32[]{:S(2)}) %collective-permute-start.21) | collective-permute-done | bytes 1048608 | tf_op jit(solution)/shard_map/ppermute | solution.py:26
  294.9 8.4 %copy.72 = bf16[8,128,2,1,2048]{4,1,0,2,3:T(8,128)(2,1)} copy(bf16[8,128,2,1,2048]{4,1,2,3,0:T(8,128)(2,1)} %bitcast_dynamic-update-slice_fusion.1) | data formatting | bytes 16777216 | tf_op jit(solution)/shard_map/stack | solution.py:35
  303.3 3.2 %fusion = f32[176,2048]{1,0:T(8,128)S(1)} fusion(bf16[2,1,1024,2048]{3,2,0,1:T(8,128)(2,1)} %bitcast.299, bf16[1,1,176,1024]{3,2,1,0:T(8,128)(2,1)S(1)} %get-tuple-element.10), kind=kOutput, calls=%fused_computation.5 | convolution fusion | flops 738197504 | bytes 5996544 | tf_op jit(solution)/shard_map/efr,erd->efd/dot_general | solution.py:120
  306.6 3.9 %fusion.4 = f32[1024,176]{0,1:T(8,128)S(1)} fusion(bf16[2,1,1024,2048]{3,2,0,1:T(8,128)(2,1)} %bitcast.300, bf16[1,176,2048]{2,1,0:T(8,128)(2,1)S(1)} %copy-done.9), kind=kOutput, calls=%fused_computation.9 | convolution fusion | flops 738197504 | bytes 5636096 | tf_op jit(solution)/shard_map/erd,efd->efr/dot_general | solution.py:117
  310.5 2.1 fusion.6
  312.6 1.6 fusion.28
  314.2 2.1 fusion.72
  316.4 3.3 %convolution_bitcast_fusion.1 = f32[1,2,176,2048]{3,2,1,0:T(8,128)} fusion(bf16[1024,2048,1]{1,0,2:T(8,128)(2,1)S(1)} %bitcast.315, bf16[1,1,176,1024]{3,2,1,0:T(8,128)(2,1)S(1)} %get-tuple-element.9, bf16[1,1,176,1024]{3,2,1,0:T(8,128)(2,1)S(1)} %get-tuple-element.8), kind=kOutput, calls=%fused_computation.10 | convolution fusion | flops 1476755456 | bytes 7798784 | tf_op jit(solution)/shard_map/ekfr,erd->ekfd/dot_general | solution.py:126
  (105 shorter events, 30.9 us)
Async XLA Ops:
  0.6 68.7 %copy-start = (bf16[1,2,176,2048]{3,2,1,0:T(8,128)(2,1)S(1)}, bf16[1,2,176,2048]{3,2,1,0:T(8,128)(2,1)}, u32[]{:S(2)}) copy-start(bf16[1,2,176,2048]{3,2,1,0:T(8,128)(2,1)} %param.14) | copy-start | bytes 4325380
  33.4 14.5 %collective-permute-start.1 = (bf16[128,1,1,2048]{3,0,2,1:T(8,128)(2,1)}, bf16[128,1,1,2048]{3,0,2,1:T(8,128)(2,1)S(1)}, u32[]{:S(2)}, u32[]{:S(2)}) collective-permute-start(bf16[128,1,1,2048]{3,0,2,1:T(8,128)(2,1)} %transpose_broadcast_in_dim_reshape_transpose_reshape.3), channel_id=1, source_target_pairs={{0,2},{1,3},{2,4},{3,5},{4,6},{5,7},{6,0},{7,1},{8,10},{9,11},{10,... | collective-permute-start | bytes 1572872 | tf_op jit(solution)/shard_map/ppermute | solution.py:26
  34.9 13.4 %collective-permute-start.2 = (bf16[128,1,1,2048]{3,0,2,1:T(8,128)(2,1)}, bf16[128,1,1,2048]{3,0,2,1:T(8,128)(2,1)}, u32[]{:S(2)}, u32[]{:S(2)}) collective-permute-start(bf16[128,1,1,2048]{3,0,2,1:T(8,128)(2,1)} %transpose_broadcast_in_dim_reshape_transpose_reshape.3), channel_id=1, source_target_pairs={{0,6},{1,7},{2,0},{3,1},{4,2},{5,3},{6,4},{7,5},{8,14},{9,15},{10,... | collective-permute-start | bytes 1572872 | tf_op jit(solution)/shard_map/ppermute | solution.py:26
  36.6 15.7 %collective-permute-start = (bf16[128,1,1,2048]{3,0,2,1:T(8,128)(2,1)}, bf16[128,1,1,2048]{3,0,2,1:T(8,128)(2,1)}, u32[]{:S(2)}, u32[]{:S(2)}) collective-permute-start(bf16[128,1,1,2048]{3,0,2,1:T(8,128)(2,1)} %transpose_broadcast_in_dim_reshape_transpose_reshape.3), channel_id=1, source_target_pairs={{0,1},{1,0},{2,3},{3,2},{4,5},{5,4},{6,7},{7,6},{8,9},{9,8},{10,11... | collective-permute-start | bytes 1572872 | tf_op jit(solution)/shard_map/ppermute | solution.py:26
  47.9 10.0 %collective-permute-start.3 = (bf16[64,1,1,2048]{3,0,2,1:T(8,128)(2,1)S(1)}, bf16[64,1,1,2048]{3,0,2,1:T(8,128)(2,1)S(1)}, u32[]{:S(2)}, u32[]{:S(2)}) collective-permute-start(bf16[64,1,1,2048]{3,0,2,1:T(8,128)(2,1)S(1)} %slice.111), channel_id=1, source_target_pairs={{0,2},{1,3},{2,4},{3,5},{4,6},{5,7},{6,0},{7,1},{8,10},{9,11},{10,... | collective-permute-start | bytes 786440 | tf_op jit(solution)/shard_map/ppermute | solution.py:26
  49.2 9.7 %collective-permute-start.4 = (bf16[64,1,1,2048]{3,0,2,1:T(8,128)(2,1)S(1)}, bf16[64,1,1,2048]{3,0,2,1:T(8,128)(2,1)S(1)}, u32[]{:S(2)}, u32[]{:S(2)}) collective-permute-start(bf16[64,1,1,2048]{3,0,2,1:T(8,128)(2,1)S(1)} %slice.112), channel_id=1, source_target_pairs={{0,6},{1,7},{2,0},{3,1},{4,2},{5,3},{6,4},{7,5},{8,14},{9,15},{10,... | collective-permute-start | bytes 786440 | tf_op jit(solution)/shard_map/ppermute | solution.py:26
  52.3 14.7 %collective-permute-start.5 = (bf16[128,1,1,2048]{3,0,2,1:T(8,128)(2,1)}, bf16[128,1,1,2048]{3,0,2,1:T(8,128)(2,1)S(1)}, u32[]{:S(2)}, u32[]{:S(2)}) collective-permute-start(bf16[128,1,1,2048]{3,0,2,1:T(8,128)(2,1)} %collective-permute-done), channel_id=1, source_target_pairs={{0,2},{1,3},{2,4},{3,5},{4,6},{5,7},{6,0},{7,1},{8,10},{9,11},{10,... | collective-permute-start | bytes 1572872 | tf_op jit(solution)/shard_map/ppermute | solution.py:26
  52.3 15.2 %collective-permute-start.6 = (bf16[128,1,1,2048]{3,0,2,1:T(8,128)(2,1)}, bf16[128,1,1,2048]{3,0,2,1:T(8,128)(2,1)S(1)}, u32[]{:S(2)}, u32[]{:S(2)}) collective-permute-start(bf16[128,1,1,2048]{3,0,2,1:T(8,128)(2,1)} %collective-permute-done), channel_id=1, source_target_pairs={{0,6},{1,7},{2,0},{3,1},{4,2},{5,3},{6,4},{7,5},{8,14},{9,15},{10,... | collective-permute-start | bytes 1572872 | tf_op jit(solution)/shard_map/ppermute | solution.py:26
  56.7 14.4 %copy-start.14 = (bf16[1,2,176,2048]{3,2,1,0:T(8,128)(2,1)S(1)}, bf16[1,2,176,2048]{3,2,1,0:T(8,128)(2,1)}, u32[]{:S(2)}) copy-start(bf16[1,2,176,2048]{3,2,1,0:T(8,128)(2,1)} %param.12) | copy-start | bytes 4325380
  59.0 10.3 %collective-permute-start.7 = (bf16[128,1,1,2048]{3,0,2,1:T(8,128)(2,1)S(1)}, bf16[128,1,1,2048]{3,0,2,1:T(8,128)(2,1)S(1)}, u32[]{:S(2)}, u32[]{:S(2)}) collective-permute-start(bf16[128,1,1,2048]{3,0,2,1:T(8,128)(2,1)S(1)} %constant_dynamic-update-slice_fusion), channel_id=1, source_target_pairs={{0,1},{1,0},{2,3},{3,2},{4,5},{5,4},{6,7},{7,6},{8,9},{9,8},{10,11... | collective-permute-start | bytes 1572872 | tf_op jit(solution)/shard_map/ppermute | solution.py:26
  69.3 3.5 %copy-start.12 = (bf16[8,128,1,1,2048]{4,1,3,2,0:T(8,128)(2,1)}, bf16[8,128,1,1,2048]{4,1,3,2,0:T(8,128)(2,1)S(1)}, u32[]{:S(2)}) copy-start(bf16[8,128,1,1,2048]{4,1,3,2,0:T(8,128)(2,1)S(1)} %bitcast_dynamic-update-slice_fusion.8) | copy-start | bytes 12582916
  71.1 2.2 copy-start.4
  71.1 2.9 copy-start.2
  72.8 1.1 copy-start.6
  74.0 2.6 copy-start.8
  78.4 21.5 %collective-permute-start.11 = (bf16[2,1,128,2048]{3,2,0,1:T(8,128)(2,1)S(1)}, bf16[2,1,128,2048]{3,2,0,1:T(8,128)(2,1)S(1)}, u32[]{:S(2)}, u32[]{:S(2)}) collective-permute-start(bf16[2,1,128,2048]{3,2,0,1:T(8,128)(2,1)S(1)} %get-tuple-element.6), channel_id=1, source_target_pairs={{0,1},{1,0},{2,3},{3,2},{4,5},{5,4},{6,7},{7,6},{8,9},{9,8},{10,11... | collective-permute-start | bytes 3145736 | tf_op jit(solution)/shard_map/ppermute | solution.py:40
  79.7 26.5 %collective-permute-start.8 = (bf16[2,1,128,2048]{3,2,0,1:T(8,128)(2,1)S(1)}, bf16[2,1,128,2048]{3,2,0,1:T(8,128)(2,1)S(1)}, u32[]{:S(2)}, u32[]{:S(2)}) collective-permute-start(bf16[2,1,128,2048]{3,2,0,1:T(8,128)(2,1)S(1)} %get-tuple-element.5), channel_id=1, source_target_pairs={{0,6},{1,7},{2,0},{3,1},{4,2},{5,3},{6,4},{7,5},{8,14},{9,15},{10,... | collective-permute-start | bytes 3145736 | tf_op jit(solution)/shard_map/ppermute | solution.py:40
  82.6 23.6 %collective-permute-start.9 = (bf16[2,1,128,2048]{3,2,0,1:T(8,128)(2,1)S(1)}, bf16[2,1,128,2048]{3,2,0,1:T(8,128)(2,1)}, u32[]{:S(2)}, u32[]{:S(2)}) collective-permute-start(bf16[2,1,128,2048]{3,2,0,1:T(8,128)(2,1)S(1)} %get-tuple-element.7), channel_id=1, source_target_pairs={{0,2},{1,3},{2,4},{3,5},{4,6},{5,7},{6,0},{7,1},{8,10},{9,11},{10,... | collective-permute-start | bytes 3145736 | tf_op jit(solution)/shard_map/ppermute | solution.py:40
  101.0 11.4 %collective-permute-start.12 = (bf16[1,1,128,2048]{3,2,0,1:T(8,128)(2,1)S(1)}, bf16[1,1,128,2048]{3,2,0,1:T(8,128)(2,1)}, u32[]{:S(2)}, u32[]{:S(2)}) collective-permute-start(bf16[1,1,128,2048]{3,2,0,1:T(8,128)(2,1)S(1)} %get-tuple-element.18), channel_id=1, source_target_pairs={{0,6},{1,7},{2,0},{3,1},{4,2},{5,3},{6,4},{7,5},{8,14},{9,15},{10,... | collective-permute-start | bytes 1572872 | tf_op jit(solution)/shard_map/ppermute | solution.py:40
  105.9 14.5 %collective-permute-start.14 = (bf16[1,1,128,2048]{3,2,0,1:T(8,128)(2,1)}, bf16[1,1,128,2048]{3,2,0,1:T(8,128)(2,1)S(1)}, u32[]{:S(2)}, u32[]{:S(2)}) collective-permute-start(bf16[1,1,128,2048]{3,2,0,1:T(8,128)(2,1)} %get-tuple-element.19), channel_id=1, source_target_pairs={{0,2},{1,3},{2,4},{3,5},{4,6},{5,7},{6,0},{7,1},{8,10},{9,11},{10,... | collective-permute-start | bytes 1572872 | tf_op jit(solution)/shard_map/ppermute | solution.py:40
  115.9 21.6 %collective-permute-start.10 = (bf16[2,1,128,2048]{3,2,0,1:T(8,128)(2,1)}, bf16[2,1,128,2048]{3,2,0,1:T(8,128)(2,1)S(1)}, u32[]{:S(2)}, u32[]{:S(2)}) collective-permute-start(bf16[2,1,128,2048]{3,2,0,1:T(8,128)(2,1)} %get-tuple-element.3), channel_id=1, source_target_pairs={{0,1},{1,0},{2,3},{3,2},{4,5},{5,4},{6,7},{7,6},{8,9},{9,8},{10,11... | collective-permute-start | bytes 3145736 | tf_op jit(solution)/shard_map/ppermute | solution.py:40
  116.6 22.2 %collective-permute-start.13 = (bf16[2,1,128,2048]{3,2,0,1:T(8,128)(2,1)}, bf16[2,1,128,2048]{3,2,0,1:T(8,128)(2,1)S(1)}, u32[]{:S(2)}, u32[]{:S(2)}) collective-permute-start(bf16[2,1,128,2048]{3,2,0,1:T(8,128)(2,1)} %get-tuple-element.4), channel_id=1, source_target_pairs={{0,6},{1,7},{2,0},{3,1},{4,2},{5,3},{6,4},{7,5},{8,14},{9,15},{10,... | collective-permute-start | bytes 3145736 | tf_op jit(solution)/shard_map/ppermute | solution.py:40
  120.7 21.6 %collective-permute-start.15 = (bf16[2,1,128,2048]{3,2,0,1:T(8,128)(2,1)S(1)}, bf16[2,1,128,2048]{3,2,0,1:T(8,128)(2,1)S(1)}, u32[]{:S(2)}, u32[]{:S(2)}) collective-permute-start(bf16[2,1,128,2048]{3,2,0,1:T(8,128)(2,1)S(1)} %fusion.12), channel_id=1, source_target_pairs={{0,2},{1,3},{2,4},{3,5},{4,6},{5,7},{6,0},{7,1},{8,10},{9,11},{10,... | collective-permute-start | bytes 3145736 | tf_op jit(solution)/shard_map/ppermute | solution.py:40
  143.0 14.0 %copy-start.3 = (bf16[128,2048]{1,0:T(8,128)(2,1)S(1)}, bf16[128,2048]{1,0:T(8,128)(2,1)}, u32[]{:S(2)}) copy-start(bf16[128,2048]{1,0:T(8,128)(2,1)} %param.8) | copy-start | bytes 1572868
  143.0 14.0 %copy-start.11 = (bf16[2048,32]{0,1:T(8,128)(2,1)S(1)}, bf16[2048,32]{0,1:T(8,128)(2,1)}, u32[]{:S(2)}) copy-start(bf16[2048,32]{0,1:T(8,128)(2,1)} %param.10) | copy-start | bytes 393220
  143.0 14.3 %copy-start.10 = (s32[128,32,4]{0,2,1:T(4,128)S(1)}, s32[128,32,4]{0,2,1:T(4,128)}, u32[]{:S(2)}) copy-start(s32[128,32,4]{0,2,1:T(4,128)} %param.11) | copy-start | bytes 196612
  148.8 37.1 %all-to-all-start.1 = ((bf16[32,2,4,2048]{3,2,1,0:T(4,128)(2,1)}), bf16[32,2,4,2048]{3,2,1,0:T(4,128)(2,1)S(1)}, u32[]{:S(2)}, u32[]{:S(2)}) async-start(bf16[32,2,4,2048]{3,2,1,0:T(4,128)(2,1)} %pad_maximum_fusion), calls=%async_computation.1 | async-start | bytes 2097152 | tf_op jit(solution)/shard_map/all_to_all | solution.py:94
  229.3 26.2 %collective-permute-start.17 = (bf16[128,2,1,2048]{3,0,1,2:T(8,128)(2,1)S(1)}, bf16[128,2,1,2048]{3,0,1,2:T(8,128)(2,1)S(1)}, u32[]{:S(2)}, u32[]{:S(2)}) collective-permute-start(bf16[128,2,1,2048]{3,0,1,2:T(8,128)(2,1)S(1)} %bitcast.306), channel_id=1, source_target_pairs={{0,2},{1,3},{2,4},{3,5},{4,6},{5,7},{6,0},{7,1},{8,10},{9,11},{10,... | collective-permute-start | bytes 3145736 | tf_op jit(solution)/shard_map/ppermute | solution.py:26
  229.8 25.9 %collective-permute-start.18 = (bf16[128,2,1,2048]{3,0,2,1:T(8,128)(2,1)S(1)}, bf16[128,2,1,2048]{3,0,2,1:T(8,128)(2,1)S(1)}, u32[]{:S(2)}, u32[]{:S(2)}) collective-permute-start(bf16[128,2,1,2048]{3,0,2,1:T(8,128)(2,1)S(1)} %bitcast.307), channel_id=1, source_target_pairs={{0,6},{1,7},{2,0},{3,1},{4,2},{5,3},{6,4},{7,5},{8,14},{9,15},{10,... | collective-permute-start | bytes 3145736 | tf_op jit(solution)/shard_map/ppermute | solution.py:26
  233.1 26.0 %collective-permute-start.16 = (bf16[128,2,1,2048]{3,0,1,2:T(8,128)(2,1)S(1)}, bf16[128,2,1,2048]{3,0,1,2:T(8,128)(2,1)S(1)}, u32[]{:S(2)}, u32[]{:S(2)}) collective-permute-start(bf16[128,2,1,2048]{3,0,1,2:T(8,128)(2,1)S(1)} %bitcast.308), channel_id=1, source_target_pairs={{0,1},{1,0},{2,3},{3,2},{4,5},{5,4},{6,7},{7,6},{8,9},{9,8},{10,11... | collective-permute-start | bytes 3145736 | tf_op jit(solution)/shard_map/ppermute | solution.py:26
  255.6 16.1 %collective-permute-start.19 = (bf16[64,2,1,2048]{3,0,1,2:T(8,128)(2,1)S(1)}, bf16[64,2,1,2048]{3,0,1,2:T(8,128)(2,1)S(1)}, u32[]{:S(2)}, u32[]{:S(2)}) collective-permute-start(bf16[64,2,1,2048]{3,0,1,2:T(8,128)(2,1)S(1)} %slice.133), channel_id=1, source_target_pairs={{0,2},{1,3},{2,4},{3,5},{4,6},{5,7},{6,0},{7,1},{8,10},{9,11},{10,... | collective-permute-start | bytes 1572872 | tf_op jit(solution)/shard_map/ppermute | solution.py:26
  255.8 16.0 %collective-permute-start.20 = (bf16[64,2,1,2048]{3,0,2,1:T(8,128)(2,1)S(1)}, bf16[64,2,1,2048]{3,0,2,1:T(8,128)(2,1)S(1)}, u32[]{:S(2)}, u32[]{:S(2)}) collective-permute-start(bf16[64,2,1,2048]{3,0,2,1:T(8,128)(2,1)S(1)} %slice.134), channel_id=1, source_target_pairs={{0,6},{1,7},{2,0},{3,1},{4,2},{5,3},{6,4},{7,5},{8,14},{9,15},{10,... | collective-permute-start | bytes 1572872 | tf_op jit(solution)/shard_map/ppermute | solution.py:26
  259.1 32.7 %collective-permute-start.21 = (bf16[128,2,1,2048]{3,0,1,2:T(8,128)(2,1)S(1)}, bf16[128,2,1,2048]{3,0,1,2:T(8,128)(2,1)S(1)}, u32[]{:S(2)}, u32[]{:S(2)}) collective-permute-start(bf16[128,2,1,2048]{3,0,1,2:T(8,128)(2,1)S(1)} %collective-permute-done.16), channel_id=1, source_target_pairs={{0,2},{1,3},{2,4},{3,5},{4,6},{5,7},{6,0},{7,1},{8,10},{9,11},{10,... | collective-permute-start | bytes 3145736 | tf_op jit(solution)/shard_map/ppermute | solution.py:26
  259.1 33.7 %collective-permute-start.22 = (bf16[128,2,1,2048]{3,0,1,2:T(8,128)(2,1)S(1)}, bf16[128,2,1,2048]{3,0,1,2:T(8,128)(2,1)S(1)}, u32[]{:S(2)}, u32[]{:S(2)}) collective-permute-start(bf16[128,2,1,2048]{3,0,1,2:T(8,128)(2,1)S(1)} %collective-permute-done.16), channel_id=1, source_target_pairs={{0,6},{1,7},{2,0},{3,1},{4,2},{5,3},{6,4},{7,5},{8,14},{9,15},{10,... | collective-permute-start | bytes 3145736 | tf_op jit(solution)/shard_map/ppermute | solution.py:26
  271.8 22.0 %collective-permute-start.23 = (bf16[128,2,1,2048]{3,0,2,1:T(8,128)(2,1)S(1)}, bf16[128,2,1,2048]{3,0,2,1:T(8,128)(2,1)S(1)}, u32[]{:S(2)}, u32[]{:S(2)}) collective-permute-start(bf16[128,2,1,2048]{3,0,2,1:T(8,128)(2,1)S(1)} %pad_maximum_fusion.2), channel_id=1, source_target_pairs={{0,1},{1,0},{2,3},{3,2},{4,5},{5,4},{6,7},{7,6},{8,9},{9,8},{10,11... | collective-permute-start | bytes 3145736 | tf_op jit(solution)/shard_map/ppermute | solution.py:26
  294.9 11.6 %copy-start.9 = (bf16[1,176,2048]{2,1,0:T(8,128)(2,1)S(1)}, bf16[1,176,2048]{2,1,0:T(8,128)(2,1)}, u32[]{:S(2)}) copy-start(bf16[1,176,2048]{2,1,0:T(8,128)(2,1)} %param.15) | copy-start | bytes 2162692
  303.3 7.2 %slice-start = ((s8[8388608]{0:T(1024)(128)(4,1)}), s8[4194304]{0:T(1024)(128)(4,1)S(1)}, s32[]{:S(2)}) async-start(s8[8388608]{0:T(1024)(128)(4,1)} %bitcast.301), calls=%async_computation.3 | async-start | bytes 8388608
  306.6 3.9 %slice-start.1 = ((s8[8388608]{0:T(1024)(128)(4,1)}), s8[4194304]{0:T(1024)(128)(4,1)S(1)}, s32[]{:S(2)}) async-start(s8[8388608]{0:T(1024)(128)(4,1)} %bitcast.301), calls=%async_computation.4 | async-start | bytes 8388608
  310.5 3.7 %copy-start.5 = (f32[1,2,176,1024]{3,2,1,0:T(8,128)S(1)}, f32[1,2,176,1024]{3,2,1,0:T(8,128)}, u32[]{:S(2)}) copy-start(f32[1,2,176,1024]{3,2,1,0:T(8,128)} %copy-done.4) | copy-start | bytes 4325380
  310.5 3.7 %copy-start.7 = (f32[1,2,176,1024]{3,2,1,0:T(8,128)S(1)}, f32[1,2,176,1024]{3,2,1,0:T(8,128)}, u32[]{:S(2)}) copy-start(f32[1,2,176,1024]{3,2,1,0:T(8,128)} %copy-done.6) | copy-start | bytes 4325380
  314.2 2.2 copy-start.13
  314.2 5.4 %copy-start.1 = (bf16[1,2,176,2048]{3,2,1,0:T(8,128)(2,1)S(1)}, bf16[1,2,176,2048]{3,2,1,0:T(8,128)(2,1)}, u32[]{:S(2)}) copy-start(bf16[1,2,176,2048]{3,2,1,0:T(8,128)(2,1)} %param.14) | copy-start | bytes 4325380

commit v3 on v2

--- a/solution.py
+++ b/solution.py
@@ -21,24 +21,26 @@
     return partner, xplus, xminus
 
 
-def tree_gather(block):
+def tree_gather(block, axis):
     partner, xplus, xminus = _perms(lax.axis_size("dp"))
     send = lambda v, perm: lax.ppermute(v, "dp", perm)
-    half = block.shape[0] // 2
+    half = block.shape[axis] // 2
+    first = lambda v: lax.slice_in_dim(v, 0, half, axis=axis)
+    second = lambda v: lax.slice_in_dim(v, half, v.shape[axis], axis=axis)
     Pb = send(block, partner)
     L = send(block, xplus)
     R = send(block, xminus)
-    O = jnp.concatenate([send(L[:half], xplus), send(R[half:], xminus)])
+    O = jnp.concatenate([send(first(L), xplus), send(second(R), xminus)], axis=axis)
     PL = send(Pb, xplus)
     PR = send(Pb, xminus)
     Q = send(O, partner)
-    return jnp.stack([block, Pb, L, R, O, PL, PR, Q])
+    return [block, Pb, L, R, O, PL, PR, Q]
 
 
 def tree_scatter_sum(acc):
     partner, xplus, xminus = _perms(lax.axis_size("dp"))
     send = lambda v, perm: lax.ppermute(v.astype(jnp.bfloat16), "dp", perm).astype(jnp.float32)
-    half = acc.shape[1] // 2
+    half = acc[0].shape[0] // 2
     a4 = acc[4] + send(acc[7], partner)
     a2 = acc[2] + jnp.concatenate([send(a4[:half], xminus), jnp.zeros_like(a4[half:])])
     a3 = acc[3] + jnp.concatenate([jnp.zeros_like(a4[:half]), send(a4[half:], xplus)])
@@ -46,31 +48,7 @@
     return acc[0] + send(a1, partner) + send(a2, xminus) + send(a3, xplus)
 
 
-def gather_dp(block):
-    k, e, r, d = block.shape
-    got = tree_gather(jnp.moveaxis(block, 2, 0))
-    return jnp.moveaxis(got.reshape(-1, k, e, d), 0, 2)
-
-
-def scatter_sum_dp(part):
-    n_dp = lax.axis_size("dp")
-    k, e, rows, d = part.shape
-    blocks = jnp.moveaxis(part.astype(jnp.float32).reshape(k, e, n_dp, rows // n_dp, d), 2, 0)
-    return tree_scatter_sum(blocks)
-
-
-def local(tokens, targets, router, picks, w_gate_up, w_down, v_gate_up, v_down):
-    highest = lax.Precision.HIGHEST
-    n_exp = lax.axis_size("expert")
-    exp_dev = w_down.shape[0]
-    onehot = picks.astype(jnp.bfloat16)
-    gates = jax.nn.sigmoid(jnp.dot(tokens, router, preferred_element_type=jnp.float32))
-    outgoing = jnp.einsum("tec,td->ecd", onehot, tokens, preferred_element_type=jnp.float32).astype(
-        jnp.bfloat16
-    )
-    arrived = lax.all_to_all(outgoing, "expert", split_axis=0, concat_axis=0, tiled=True)
-    rows = gather_dp(regroup(arrived, exp_dev)[None])[0]
-    scale = 1.0 / math.sqrt(rows.shape[1])
+def forward_group(rows, w_gate_up, w_down, v_gate_up, v_down):
     primal = jnp.einsum("ekfd,erd->ekfr", w_gate_up, rows, preferred_element_type=jnp.float32)
     tangent = jnp.einsum("ekfd,erd->ekfr", v_gate_up, rows, preferred_element_type=jnp.float32)
     gate_pre, up_pre = (primal[:, 0], primal[:, 1])
@@ -86,7 +64,50 @@
     part_dot = jnp.einsum(
         "efr,efd->erd", hidden_dot, w_down, preferred_element_type=jnp.float32
     ) + jnp.einsum("efr,efd->erd", hidden, v_down, preferred_element_type=jnp.float32)
-    own_both = scatter_sum_dp(jnp.stack([part_out, part_dot]))
+    saved = (rows, up_pre, gate_dot, up_dot, active, slope, curve, act_dot, hidden, hidden_dot)
+    return jnp.stack([part_out, part_dot]), saved
+
+
+def backward_group(cot_blocks, saved, w_down, v_down):
+    rows, up_pre, gate_dot, up_dot, active, slope, curve, act_dot, hidden, hidden_dot = saved
+    both = jnp.concatenate(cot_blocks, axis=2)
+    cot_rows, cdot_rows = (both[0], both[1])
+    grad_hid = jnp.einsum("erd,efd->efr", cot_rows, w_down, preferred_element_type=jnp.float32)
+    grad_hdot = jnp.einsum(
+        "erd,efd->efr", cdot_rows, w_down, preferred_element_type=jnp.float32
+    ) + jnp.einsum("erd,efd->efr", cot_rows, v_down, preferred_element_type=jnp.float32)
+    hvp_down = jnp.einsum(
+        "efr,erd->efd", hidden_dot, cot_rows, preferred_element_type=jnp.float32
+    ) + jnp.einsum("efr,erd->efd", hidden, cdot_rows, preferred_element_type=jnp.float32)
+    gate_term = (
+        (grad_hdot * up_pre + grad_hid * up_dot) * slope + grad_hid * up_pre * curve * gate_dot
+    ).astype(jnp.bfloat16)
+    up_term = (grad_hdot * active + grad_hid * act_dot).astype(jnp.bfloat16)
+    both_terms = jnp.stack([gate_term, up_term], axis=1)
+    hvp_gate_up = jnp.einsum("ekfr,erd->ekfd", both_terms, rows, preferred_element_type=jnp.float32)
+    return hvp_gate_up, hvp_down
+
+
+def local(tokens, targets, router, picks, w_gate_up, w_down, v_gate_up, v_down):
+    highest = lax.Precision.HIGHEST
+    n_exp = lax.axis_size("expert")
+    exp_dev = w_down.shape[0]
+    onehot = picks.astype(jnp.bfloat16)
+    gates = jax.nn.sigmoid(jnp.dot(tokens, router, preferred_element_type=jnp.float32))
+    outgoing = jnp.einsum("tec,td->ecd", onehot, tokens, preferred_element_type=jnp.float32).astype(
+        jnp.bfloat16
+    )
+    arrived = lax.all_to_all(outgoing, "expert", split_axis=0, concat_axis=0, tiled=True)
+    row_blocks = tree_gather(regroup(arrived, exp_dev), 1)
+    block_rows = row_blocks[0].shape[1]
+    scale = 1.0 / math.sqrt(block_rows * len(row_blocks))
+    groups = (row_blocks[:4], row_blocks[4:])
+    parts, saved = [], []
+    for blocks in groups:
+        part, kept = forward_group(jnp.concatenate(blocks, axis=1), w_gate_up, w_down, v_gate_up, v_down)
+        parts += [part[:, :, i * block_rows:(i + 1) * block_rows] for i in range(len(blocks))]
+        saved.append(kept)
+    own_both = tree_scatter_sum(parts)
     back_both = jnp.stack(
         [regroup(own_both[0].astype(jnp.bfloat16), n_exp), regroup(own_both[1].astype(jnp.bfloat16), n_exp)],
         axis=1,
@@ -109,22 +130,10 @@
         jnp.stack([cot_send, cdot_send], axis=1), "expert", split_axis=0, concat_axis=0, tiled=True
     )
     own_both = jnp.stack([regroup(both_got[:, 0], exp_dev), regroup(both_got[:, 1], exp_dev)])
-    both_rows = gather_dp(own_both)
-    cot_rows, cdot_rows = (both_rows[0], both_rows[1])
-    grad_hid = jnp.einsum("erd,efd->efr", cot_rows, w_down, preferred_element_type=jnp.float32)
-    grad_hdot = jnp.einsum(
-        "erd,efd->efr", cdot_rows, w_down, preferred_element_type=jnp.float32
-    ) + jnp.einsum("erd,efd->efr", cot_rows, v_down, preferred_element_type=jnp.float32)
-    hvp_down = jnp.einsum(
-        "efr,erd->efd", hidden_dot, cot_rows, preferred_element_type=jnp.float32
-    ) + jnp.einsum("efr,erd->efd", hidden, cdot_rows, preferred_element_type=jnp.float32)
-    gate_term = (
-        (grad_hdot * up_pre + grad_hid * up_dot) * slope + grad_hid * up_pre * curve * gate_dot
-    ).astype(jnp.bfloat16)
-    up_term = (grad_hdot * active + grad_hid * act_dot).astype(jnp.bfloat16)
-    both_terms = jnp.stack([gate_term, up_term], axis=1)
-    hvp_gate_up = jnp.einsum("ekfr,erd->ekfd", both_terms, rows, preferred_element_type=jnp.float32)
-    return (mixed, hvp_gate_up, hvp_down)
+    cot_blocks = tree_gather(own_both, 0)
+    hvp_gate_up, hvp_down = backward_group(cot_blocks[:4], saved[0], w_down, v_down)
+    late_gate_up, late_down = backward_group(cot_blocks[4:], saved[1], w_down, v_down)
+    return (mixed, hvp_gate_up + late_gate_up, hvp_down + late_down)
 
 
 def solution(mesh):

time: 326 us -> 310 us (0.951)
  the two profiles are of different devices: /device:TPU:16 before, /device:TPU:56 now
where the time goes in v3:
time: 310 us; the launch traced here: 304 us
  waiting for transfers between devices  144 us (46%)
  blocking collectives  61.9 us (20%)
  starting transfers between devices  43.8 us (14%)
  matrix products  27.8 us (9%)
  local copies, waits for them, and re-layouts  18.3 us (6%)
  other arithmetic  7 us (2%)
    ppermute x16, waiting for transfers between devices, tree_gather(): send = lambda v, perm: lax.ppermute(v, 'dp', perm)  70.7 us
    ppermute x8, waiting for transfers between devices, tree_scatter_sum(): lax.ppermute(v.astype(jnp.bfloat16), 'dp', perm).astype(jnp.float32)  46.4 us
    all_to_all x1, blocking collectives, local(): lax.all_to_all(jnp.stack([cot_send, cdot_send], axis=1), 'expert', split_...  34.1 us
    all_to_all x1, blocking collectives, local(): lax.all_to_all(outgoing, 'expert', split_axis=0, concat_axis=0, tiled=True)  27.8 us
    all_to_all x1, waiting for transfers between devices, local(): lax.all_to_all(back_both, 'expert', split_axis=0, concat_axis=0, tiled=True)  26.7 us
    ppermute x16, starting transfers between devices, tree_gather(): send = lambda v, perm: lax.ppermute(v, 'dp', perm)  22.2 us
    all_to_all x1, starting transfers between devices, local(): lax.all_to_all(back_both, 'expert', split_axis=0, concat_axis=0, tiled=True)  11.2 us
    ppermute x8, starting transfers between devices, tree_scatter_sum(): lax.ppermute(v.astype(jnp.bfloat16), 'dp', perm).astype(jnp.float32)  10.4 us
  transfers between devices with their start and end apart: 25, of which 17 were waited for; matrix products, arithmetic and copies ran while one was open for 4% of the time, Pallas kernels for 0%

profile of v3, /device:TPU:56, one launch (start us, length us, event | category | flops | bytes accessed | tf_op | source)
XLA Modules:
  0.0 304.2 jit_solution(6113020039996239052)
XLA Ops:
  1.6 1.3 convolution_convert_fusion.2
  3.4 27.8 %all_to_all.15 = bf16[32,4,2048]{2,1,0:T(4,128)(2,1)S(1)} all-to-all(bf16[32,4,2048]{2,1,0:T(4,128)(2,1)S(1)} %copy.27), channel_id=1, replica_groups=mesh['expert'=32,'dp'=8] {'expert'}, dimensions={0} | all-to-all | bytes 1048576 | tf_op jit(solution)/shard_map/all_to_all | solution.py:100
  31.3 1.6 collective-permute-start.1
  32.8 1.7 collective-permute-start.2
  35.3 10.2 %collective-permute-done.1 = bf16[1,128,2048]{2,1,0:T(8,128)(2,1)S(1)} collective-permute-done((bf16[1,128,2048]{2,1,0:T(8,128)(2,1)S(1)}, bf16[1,128,2048]{2,1,0:T(8,128)(2,1)S(1)}, u32[]{:S(2)}, u32[]{:S(2)}) %collective-permute-start.1) | collective-permute-done | bytes 524320 | tf_op jit(solution)/shard_map/ppermute | solution.py:26
  45.9 3.0 collective-permute-start.4
  49.0 3.2 %collective-permute-start.6 = (bf16[1,128,2048]{2,1,0:T(8,128)(2,1)S(1)}, bf16[1,128,2048]{2,1,0:T(8,128)(2,1)S(1)}, u32[]{:S(2)}, u32[]{:S(2)}) collective-permute-start(bf16[1,128,2048]{2,1,0:T(8,128)(2,1)S(1)} %collective-permute-done), channel_id=1, source_target_pairs={{0,6},{1,7},{2,0},{3,1},{4,2},{5,3},{6,4},{7,5},{8,14},{9,15},{10,... | collective-permute-start | bytes 1572872 | tf_op jit(solution)/shard_map/ppermute | solution.py:26
  52.2 3.9 %collective-permute-done.3 = bf16[1,64,2048]{2,1,0:T(8,128)(2,1)S(1)} collective-permute-done((bf16[1,64,2048]{2,1,0:T(8,128)(2,1)S(1)}, bf16[1,64,2048]{2,1,0:T(8,128)(2,1)S(1)}, u32[]{:S(2)}, u32[]{:S(2)}) %collective-permute-start.3) | collective-permute-done | bytes 262176 | tf_op jit(solution)/shard_map/ppermute | solution.py:26
  57.2 7.3 %collective-permute-done.5 = bf16[1,128,2048]{2,1,0:T(8,128)(2,1)S(1)} collective-permute-done((bf16[1,128,2048]{2,1,0:T(8,128)(2,1)S(1)}, bf16[1,128,2048]{2,1,0:T(8,128)(2,1)S(1)}, u32[]{:S(2)}, u32[]{:S(2)}) %collective-permute-start.5) | collective-permute-done | bytes 524320 | tf_op jit(solution)/shard_map/ppermute | solution.py:26
  68.9 1.1 copy-done.2
  77.7 3.4 %collective-permute-start.8 = (bf16[2,1,128,2048]{3,2,1,0:T(8,128)(2,1)S(1)}, bf16[2,1,128,2048]{3,2,1,0:T(8,128)(2,1)S(1)}, u32[]{:S(2)}, u32[]{:S(2)}) collective-permute-start(bf16[2,1,128,2048]{3,2,1,0:T(8,128)(2,1)S(1)} %get-tuple-element.6), channel_id=1, source_target_pairs={{0,6},{1,7},{2,0},{3,1},{4,2},{5,3},{6,4},{7,5},{8,14},{9,15},{10,... | collective-permute-start | bytes 3145736 | tf_op jit(solution)/shard_map/ppermute | solution.py:42
  81.1 14.3 %collective-permute-done.11 = bf16[2,1,128,2048]{3,2,1,0:T(8,128)(2,1)S(1)} collective-permute-done((bf16[2,1,128,2048]{3,2,1,0:T(8,128)(2,1)S(1)}, bf16[2,1,128,2048]{3,2,1,0:T(8,128)(2,1)S(1)}, u32[]{:S(2)}, u32[]{:S(2)}) %collective-permute-start.11) | collective-permute-done | bytes 1048608 | tf_op jit(solution)/shard_map/ppermute | solution.py:42
  95.8 2.8 collective-permute-start.12
  100.3 4.4 %collective-permute-done.8 = bf16[2,1,128,2048]{3,2,1,0:T(8,128)(2,1)S(1)} collective-permute-done((bf16[2,1,128,2048]{3,2,1,0:T(8,128)(2,1)S(1)}, bf16[2,1,128,2048]{3,2,1,0:T(8,128)(2,1)S(1)}, u32[]{:S(2)}, u32[]{:S(2)}) %collective-permute-start.8) | collective-permute-done | bytes 1048608 | tf_op jit(solution)/shard_map/ppermute | solution.py:42
  104.7 3.6 %collective-permute-done.9 = bf16[2,1,128,2048]{3,2,1,0:T(8,128)(2,1)S(1)} collective-permute-done((bf16[2,1,128,2048]{3,2,1,0:T(8,128)(2,1)S(1)}, bf16[2,1,128,2048]{3,2,1,0:T(8,128)(2,1)S(1)}, u32[]{:S(2)}, u32[]{:S(2)}) %collective-permute-start.9) | collective-permute-done | bytes 1048608 | tf_op jit(solution)/shard_map/ppermute | solution.py:42
  108.3 2.3 collective-permute-done.12
  110.6 3.4 %collective-permute-done.14 = bf16[1,1,128,2048]{3,2,1,0:T(8,128)(2,1)S(1)} collective-permute-done((bf16[1,1,128,2048]{3,2,1,0:T(8,128)(2,1)S(1)}, bf16[1,1,128,2048]{3,2,1,0:T(8,128)(2,1)S(1)}, u32[]{:S(2)}, u32[]{:S(2)}) %collective-permute-start.14) | collective-permute-done | bytes 524320 | tf_op jit(solution)/shard_map/ppermute | solution.py:42
  115.0 1.2 collective-permute-start.10
  116.4 1.7 collective-permute-start.15
  118.2 16.5 %collective-permute-done.10 = bf16[2,1,128,2048]{3,2,1,0:T(8,128)(2,1)S(1)} collective-permute-done((bf16[2,1,128,2048]{3,2,1,0:T(8,128)(2,1)S(1)}, bf16[2,1,128,2048]{3,2,1,0:T(8,128)(2,1)S(1)}, u32[]{:S(2)}, u32[]{:S(2)}) %collective-permute-start.10) | collective-permute-done | bytes 1048608 | tf_op jit(solution)/shard_map/ppermute | solution.py:42
  135.2 1.5 collective-permute-done.15
  137.4 1.0 fusion.151
  138.4 1.2 convert_element_type.167
  139.7 1.2 convert_element_type.168
  140.9 1.7 pad_maximum_fusion.4
  142.6 11.2 %all-to-all-start.1 = ((bf16[32,2,4,2048]{3,2,1,0:T(4,128)(2,1)}), bf16[32,2,4,2048]{3,2,1,0:T(4,128)(2,1)S(1)}, u32[]{:S(2)}, u32[]{:S(2)}) async-start(bf16[32,2,4,2048]{3,2,1,0:T(4,128)(2,1)} %pad_maximum_fusion.4), calls=%async_computation.1 | async-start | bytes 2097152 | tf_op jit(solution)/shard_map/all_to_all | solution.py:115
  153.8 1.3 fusion.69
  155.2 26.7 %all-to-all-done.1 = bf16[32,2,4,2048]{3,2,1,0:T(4,128)(2,1)S(1)} async-done(((bf16[32,2,4,2048]{3,2,1,0:T(4,128)(2,1)}), bf16[32,2,4,2048]{3,2,1,0:T(4,128)(2,1)S(1)}, u32[]{:S(2)}, u32[]{:S(2)}) %all-to-all-start.1) | async-done | bytes 1048608 | tf_op jit(solution)/shard_map/all_to_all | solution.py:115
  182.4 1.6 fusion.153
  184.8 1.0 fusion.7
  185.8 1.1 fusion.6
  187.8 34.1 %all_to_all.16 = bf16[32,2,4,2048]{3,2,1,0:T(4,128)(2,1)S(1)} all-to-all(bf16[32,2,4,2048]{3,2,1,0:T(4,128)(2,1)S(1)} %copy.36), channel_id=1, replica_groups=mesh['expert'=32,'dp'=8] {'expert'}, dimensions={0} | all-to-all | bytes 2097152 | tf_op jit(solution)/shard_map/all_to_all | solution.py:129
  221.9 1.5 fusion.149
  223.4 2.0 stack_reshape_transpose_reshape_squeeze.6
  225.4 1.1 constant_dynamic-update-slice_fusion.6
  226.5 2.0 stack_reshape_transpose_reshape_squeeze.7
  228.5 1.1 constant_dynamic-update-slice_fusion.5
  229.9 3.0 collective-permute-start.18
  233.0 22.9 %collective-permute-done.17 = bf16[2,1,128,2048]{3,2,1,0:T(8,128)(2,1)S(1)} collective-permute-done((bf16[2,1,128,2048]{3,2,1,0:T(8,128)(2,1)S(1)}, bf16[2,1,128,2048]{3,2,1,0:T(8,128)(2,1)S(1)}, u32[]{:S(2)}, u32[]{:S(2)}) %collective-permute-start.17) | collective-permute-done | bytes 1048608 | tf_op jit(solution)/shard_map/ppermute | solution.py:26
  256.1 3.3 %collective-permute-start.20 = (bf16[1,1,128,2048]{3,2,1,0:T(8,128)(2,1)S(1)}, bf16[1,1,128,2048]{3,2,1,0:T(8,128)(2,1)S(1)}, u32[]{:S(2)}, u32[]{:S(2)}) collective-permute-start(bf16[1,1,128,2048]{3,2,1,0:T(8,128)(2,1)S(1)} %slice.167), channel_id=1, source_target_pairs={{0,6},{1,7},{2,0},{3,1},{4,2},{5,3},{6,4},{7,5},{8,14},{9,15},{10,... | collective-permute-start | bytes 1572872 | tf_op jit(solution)/shard_map/ppermute | solution.py:26
  259.4 3.2 %collective-permute-start.22 = (bf16[2,1,128,2048]{3,2,1,0:T(8,128)(2,1)S(1)}, bf16[2,1,128,2048]{3,2,1,0:T(8,128)(2,1)S(1)}, u32[]{:S(2)}, u32[]{:S(2)}) collective-permute-start(bf16[2,1,128,2048]{3,2,1,0:T(8,128)(2,1)S(1)} %collective-permute-done.16), channel_id=1, source_target_pairs={{0,6},{1,7},{2,0},{3,1},{4,2},{5,3},{6,4},{7,5},{8,14},{9,15},{10,... | collective-permute-start | bytes 3145736 | tf_op jit(solution)/shard_map/ppermute | solution.py:26
  264.5 7.6 %collective-permute-done.19 = bf16[1,1,128,2048]{3,2,1,0:T(8,128)(2,1)S(1)} collective-permute-done((bf16[1,1,128,2048]{3,2,1,0:T(8,128)(2,1)S(1)}, bf16[1,1,128,2048]{3,2,1,0:T(8,128)(2,1)S(1)}, u32[]{:S(2)}, u32[]{:S(2)}) %collective-permute-start.19) | collective-permute-done | bytes 524320 | tf_op jit(solution)/shard_map/ppermute | solution.py:26
  274.8 1.1 fusion.139
  275.9 16.8 %collective-permute-done.21 = bf16[2,1,128,2048]{3,2,1,0:T(8,128)(2,1)S(1)} collective-permute-done((bf16[2,1,128,2048]{3,2,1,0:T(8,128)(2,1)S(1)}, bf16[2,1,128,2048]{3,2,1,0:T(8,128)(2,1)S(1)}, u32[]{:S(2)}, u32[]{:S(2)}) %collective-permute-start.21) | collective-permute-done | bytes 1048608 | tf_op jit(solution)/shard_map/ppermute | solution.py:26
  292.6 1.2 collective-permute-done.23
  297.1 1.1 fusion.138
  298.2 1.7 fusion.3
  301.5 2.5 fusion.1
  (126 shorter events, 32.4 us)
Async XLA Ops:
  0.6 65.0 %copy-start = (bf16[1,2,176,2048]{3,2,1,0:T(8,128)(2,1)S(1)}, bf16[1,2,176,2048]{3,2,1,0:T(8,128)(2,1)}, u32[]{:S(2)}) copy-start(bf16[1,2,176,2048]{3,2,1,0:T(8,128)(2,1)} %param.12) | copy-start | bytes 4325380
  31.3 33.3 %copy-start.14 = (bf16[1,128,2048]{2,1,0:T(8,128)(2,1)}, bf16[1,128,2048]{2,1,0:T(8,128)(2,1)S(1)}, u32[]{:S(2)}) copy-start(bf16[1,128,2048]{2,1,0:T(8,128)(2,1)S(1)} %reshape_transpose_reshape.3) | copy-start | bytes 1572868
  31.3 14.2 %collective-permute-start.1 = (bf16[1,128,2048]{2,1,0:T(8,128)(2,1)S(1)}, bf16[1,128,2048]{2,1,0:T(8,128)(2,1)S(1)}, u32[]{:S(2)}, u32[]{:S(2)}) collective-permute-start(bf16[1,128,2048]{2,1,0:T(8,128)(2,1)S(1)} %reshape_transpose_reshape.3), channel_id=1, source_target_pairs={{0,2},{1,3},{2,4},{3,5},{4,6},{5,7},{6,0},{7,1},{8,10},{9,11},{10,... | collective-permute-start | bytes 1572872 | tf_op jit(solution)/shard_map/ppermute | solution.py:26
  32.8 13.1 %collective-permute-start.2 = (bf16[1,128,2048]{2,1,0:T(8,128)(2,1)S(1)}, bf16[1,128,2048]{2,1,0:T(8,128)(2,1)S(1)}, u32[]{:S(2)}, u32[]{:S(2)}) collective-permute-start(bf16[1,128,2048]{2,1,0:T(8,128)(2,1)S(1)} %reshape_transpose_reshape.3), channel_id=1, source_target_pairs={{0,6},{1,7},{2,0},{3,1},{4,2},{5,3},{6,4},{7,5},{8,14},{9,15},{10,... | collective-permute-start | bytes 1572872 | tf_op jit(solution)/shard_map/ppermute | solution.py:26
  34.6 14.4 %collective-permute-start = (bf16[1,128,2048]{2,1,0:T(8,128)(2,1)S(1)}, bf16[1,128,2048]{2,1,0:T(8,128)(2,1)S(1)}, u32[]{:S(2)}, u32[]{:S(2)}) collective-permute-start(bf16[1,128,2048]{2,1,0:T(8,128)(2,1)S(1)} %reshape_transpose_reshape.3), channel_id=1, source_target_pairs={{0,1},{1,0},{2,3},{3,2},{4,5},{5,4},{6,7},{7,6},{8,9},{9,8},{10,11... | collective-permute-start | bytes 1572872 | tf_op jit(solution)/shard_map/ppermute | solution.py:26
  45.5 30.2 %copy-start.19 = (bf16[1,128,2048]{2,1,0:T(8,128)(2,1)}, bf16[1,128,2048]{2,1,0:T(8,128)(2,1)S(1)}, u32[]{:S(2)}) copy-start(bf16[1,128,2048]{2,1,0:T(8,128)(2,1)S(1)} %collective-permute-done.1) | copy-start | bytes 1572868
  45.5 10.5 %collective-permute-start.3 = (bf16[1,64,2048]{2,1,0:T(8,128)(2,1)S(1)}, bf16[1,64,2048]{2,1,0:T(8,128)(2,1)S(1)}, u32[]{:S(2)}, u32[]{:S(2)}) collective-permute-start(bf16[1,64,2048]{2,1,0:T(8,128)(2,1)S(1)} %slice.143), channel_id=1, source_target_pairs={{0,2},{1,3},{2,4},{3,5},{4,6},{5,7},{6,0},{7,1},{8,10},{9,11},{10,... | collective-permute-start | bytes 786440 | tf_op jit(solution)/shard_map/ppermute | solution.py:26
  45.9 29.8 %copy-start.21 = (bf16[1,128,2048]{2,1,0:T(8,128)(2,1)}, bf16[1,128,2048]{2,1,0:T(8,128)(2,1)S(1)}, u32[]{:S(2)}) copy-start(bf16[1,128,2048]{2,1,0:T(8,128)(2,1)S(1)} %collective-permute-done.2) | copy-start | bytes 1572868
  45.9 10.1 %collective-permute-start.4 = (bf16[1,64,2048]{2,1,0:T(8,128)(2,1)S(1)}, bf16[1,64,2048]{2,1,0:T(8,128)(2,1)S(1)}, u32[]{:S(2)}, u32[]{:S(2)}) collective-permute-start(bf16[1,64,2048]{2,1,0:T(8,128)(2,1)S(1)} %slice.144), channel_id=1, source_target_pairs={{0,6},{1,7},{2,0},{3,1},{4,2},{5,3},{6,4},{7,5},{8,14},{9,15},{10,... | collective-permute-start | bytes 786440 | tf_op jit(solution)/shard_map/ppermute | solution.py:26
  49.0 15.6 %copy-start.25 = (bf16[1,128,2048]{2,1,0:T(8,128)(2,1)}, bf16[1,128,2048]{2,1,0:T(8,128)(2,1)S(1)}, u32[]{:S(2)}) copy-start(bf16[1,128,2048]{2,1,0:T(8,128)(2,1)S(1)} %collective-permute-done) | copy-start | bytes 1572868
  49.0 15.5 %collective-permute-start.5 = (bf16[1,128,2048]{2,1,0:T(8,128)(2,1)S(1)}, bf16[1,128,2048]{2,1,0:T(8,128)(2,1)S(1)}, u32[]{:S(2)}, u32[]{:S(2)}) collective-permute-start(bf16[1,128,2048]{2,1,0:T(8,128)(2,1)S(1)} %collective-permute-done), channel_id=1, source_target_pairs={{0,2},{1,3},{2,4},{3,5},{4,6},{5,7},{6,0},{7,1},{8,10},{9,11},{10,... | collective-permute-start | bytes 1572872 | tf_op jit(solution)/shard_map/ppermute | solution.py:26
  49.0 15.6 %collective-permute-start.6 = (bf16[1,128,2048]{2,1,0:T(8,128)(2,1)S(1)}, bf16[1,128,2048]{2,1,0:T(8,128)(2,1)S(1)}, u32[]{:S(2)}, u32[]{:S(2)}) collective-permute-start(bf16[1,128,2048]{2,1,0:T(8,128)(2,1)S(1)} %collective-permute-done), channel_id=1, source_target_pairs={{0,6},{1,7},{2,0},{3,1},{4,2},{5,3},{6,4},{7,5},{8,14},{9,15},{10,... | collective-permute-start | bytes 1572872 | tf_op jit(solution)/shard_map/ppermute | solution.py:26
  56.1 9.4 %collective-permute-start.7 = (bf16[1,128,2048]{2,1,0:T(8,128)(2,1)S(1)}, bf16[1,128,2048]{2,1,0:T(8,128)(2,1)S(1)}, u32[]{:S(2)}, u32[]{:S(2)}) collective-permute-start(bf16[1,128,2048]{2,1,0:T(8,128)(2,1)S(1)} %pad_maximum_fusion.6), channel_id=1, source_target_pairs={{0,1},{1,0},{2,3},{3,2},{4,5},{5,4},{6,7},{7,6},{8,9},{9,8},{10,11... | collective-permute-start | bytes 1572872 | tf_op jit(solution)/shard_map/ppermute | solution.py:26
  65.6 1.3 copy-start.4
  65.6 2.1 copy-start.24
  68.7 2.1 copy-start.8
  68.7 1.4 copy-start.2
  73.5 1.3 copy-start.15
  73.5 1.3 copy-start.26
  73.9 21.5 %collective-permute-start.11 = (bf16[2,1,128,2048]{3,2,1,0:T(8,128)(2,1)S(1)}, bf16[2,1,128,2048]{3,2,1,0:T(8,128)(2,1)S(1)}, u32[]{:S(2)}, u32[]{:S(2)}) collective-permute-start(bf16[2,1,128,2048]{3,2,1,0:T(8,128)(2,1)S(1)} %get-tuple-element.7), channel_id=1, source_target_pairs={{0,1},{1,0},{2,3},{3,2},{4,5},{5,4},{6,7},{7,6},{8,9},{9,8},{10,11... | collective-permute-start | bytes 3145736 | tf_op jit(solution)/shard_map/ppermute | solution.py:42
  77.7 27.0 %collective-permute-start.8 = (bf16[2,1,128,2048]{3,2,1,0:T(8,128)(2,1)S(1)}, bf16[2,1,128,2048]{3,2,1,0:T(8,128)(2,1)S(1)}, u32[]{:S(2)}, u32[]{:S(2)}) collective-permute-start(bf16[2,1,128,2048]{3,2,1,0:T(8,128)(2,1)S(1)} %get-tuple-element.6), channel_id=1, source_target_pairs={{0,6},{1,7},{2,0},{3,1},{4,2},{5,3},{6,4},{7,5},{8,14},{9,15},{10,... | collective-permute-start | bytes 3145736 | tf_op jit(solution)/shard_map/ppermute | solution.py:42
  81.1 27.2 %collective-permute-start.9 = (bf16[2,1,128,2048]{3,2,1,0:T(8,128)(2,1)S(1)}, bf16[2,1,128,2048]{3,2,1,0:T(8,128)(2,1)S(1)}, u32[]{:S(2)}, u32[]{:S(2)}) collective-permute-start(bf16[2,1,128,2048]{3,2,1,0:T(8,128)(2,1)S(1)} %get-tuple-element.8), channel_id=1, source_target_pairs={{0,2},{1,3},{2,4},{3,5},{4,6},{5,7},{6,0},{7,1},{8,10},{9,11},{10,... | collective-permute-start | bytes 3145736 | tf_op jit(solution)/shard_map/ppermute | solution.py:42
  95.8 14.8 %collective-permute-start.12 = (bf16[1,1,128,2048]{3,2,1,0:T(8,128)(2,1)S(1)}, bf16[1,1,128,2048]{3,2,1,0:T(8,128)(2,1)S(1)}, u32[]{:S(2)}, u32[]{:S(2)}) collective-permute-start(bf16[1,1,128,2048]{3,2,1,0:T(8,128)(2,1)S(1)} %get-tuple-element.19), channel_id=1, source_target_pairs={{0,6},{1,7},{2,0},{3,1},{4,2},{5,3},{6,4},{7,5},{8,14},{9,15},{10,... | collective-permute-start | bytes 1572872 | tf_op jit(solution)/shard_map/ppermute | solution.py:42
  98.6 15.4 %collective-permute-start.14 = (bf16[1,1,128,2048]{3,2,1,0:T(8,128)(2,1)S(1)}, bf16[1,1,128,2048]{3,2,1,0:T(8,128)(2,1)S(1)}, u32[]{:S(2)}, u32[]{:S(2)}) collective-permute-start(bf16[1,1,128,2048]{3,2,1,0:T(8,128)(2,1)S(1)} %get-tuple-element.20), channel_id=1, source_target_pairs={{0,2},{1,3},{2,4},{3,5},{4,6},{5,7},{6,0},{7,1},{8,10},{9,11},{10,... | collective-permute-start | bytes 1572872 | tf_op jit(solution)/shard_map/ppermute | solution.py:42
  115.0 19.7 %collective-permute-start.10 = (bf16[2,1,128,2048]{3,2,1,0:T(8,128)(2,1)S(1)}, bf16[2,1,128,2048]{3,2,1,0:T(8,128)(2,1)S(1)}, u32[]{:S(2)}, u32[]{:S(2)}) collective-permute-start(bf16[2,1,128,2048]{3,2,1,0:T(8,128)(2,1)S(1)} %get-tuple-element.3), channel_id=1, source_target_pairs={{0,1},{1,0},{2,3},{3,2},{4,5},{5,4},{6,7},{7,6},{8,9},{9,8},{10,11... | collective-permute-start | bytes 3145736 | tf_op jit(solution)/shard_map/ppermute | solution.py:42
  116.1 19.0 %collective-permute-start.13 = (bf16[2,1,128,2048]{3,2,1,0:T(8,128)(2,1)S(1)}, bf16[2,1,128,2048]{3,2,1,0:T(8,128)(2,1)S(1)}, u32[]{:S(2)}, u32[]{:S(2)}) collective-permute-start(bf16[2,1,128,2048]{3,2,1,0:T(8,128)(2,1)S(1)} %get-tuple-element.5), channel_id=1, source_target_pairs={{0,6},{1,7},{2,0},{3,1},{4,2},{5,3},{6,4},{7,5},{8,14},{9,15},{10,... | collective-permute-start | bytes 3145736 | tf_op jit(solution)/shard_map/ppermute | solution.py:42
  116.4 20.2 %collective-permute-start.15 = (bf16[2,1,128,2048]{3,2,1,0:T(8,128)(2,1)S(1)}, bf16[2,1,128,2048]{3,2,1,0:T(8,128)(2,1)S(1)}, u32[]{:S(2)}, u32[]{:S(2)}) collective-permute-start(bf16[2,1,128,2048]{3,2,1,0:T(8,128)(2,1)S(1)} %get-tuple-element.4), channel_id=1, source_target_pairs={{0,2},{1,3},{2,4},{3,5},{4,6},{5,7},{6,0},{7,1},{8,10},{9,11},{10,... | collective-permute-start | bytes 3145736 | tf_op jit(solution)/shard_map/ppermute | solution.py:42
  140.9 12.9 %copy-start.23 = (bf16[2048,32]{0,1:T(8,128)(2,1)S(1)}, bf16[2048,32]{0,1:T(8,128)(2,1)}, u32[]{:S(2)}) copy-start(bf16[2048,32]{0,1:T(8,128)(2,1)} %param.10) | copy-start | bytes 393220
  140.9 14.2 %copy-start.18 = (s32[128,32,4]{0,2,1:T(4,128)S(1)}, s32[128,32,4]{0,2,1:T(4,128)}, u32[]{:S(2)}) copy-start(s32[128,32,4]{0,2,1:T(4,128)} %param.11) | copy-start | bytes 196612
  142.6 39.3 %all-to-all-start.1 = ((bf16[32,2,4,2048]{3,2,1,0:T(4,128)(2,1)}), bf16[32,2,4,2048]{3,2,1,0:T(4,128)(2,1)S(1)}, u32[]{:S(2)}, u32[]{:S(2)}) async-start(bf16[32,2,4,2048]{3,2,1,0:T(4,128)(2,1)} %pad_maximum_fusion.4), calls=%async_computation.1 | async-start | bytes 2097152 | tf_op jit(solution)/shard_map/all_to_all | solution.py:115
  184.0 1.8 copy-start.17
  229.5 26.3 %collective-permute-start.17 = (bf16[2,1,128,2048]{3,2,1,0:T(8,128)(2,1)S(1)}, bf16[2,1,128,2048]{3,2,1,0:T(8,128)(2,1)S(1)}, u32[]{:S(2)}, u32[]{:S(2)}) collective-permute-start(bf16[2,1,128,2048]{3,2,1,0:T(8,128)(2,1)S(1)} %constant_dynamic-update-slice_fusion.5), channel_id=1, source_target_pairs={{0,2},{1,3},{2,4},{3,5},{4,6},{5,7},{6,0},{7,1},{8,10},{9,11},{10,... | collective-permute-start | bytes 3145736 | tf_op jit(solution)/shard_map/ppermute | solution.py:26
  229.9 26.2 %collective-permute-start.18 = (bf16[2,1,128,2048]{3,2,1,0:T(8,128)(2,1)S(1)}, bf16[2,1,128,2048]{3,2,1,0:T(8,128)(2,1)S(1)}, u32[]{:S(2)}, u32[]{:S(2)}) collective-permute-start(bf16[2,1,128,2048]{3,2,1,0:T(8,128)(2,1)S(1)} %constant_dynamic-update-slice_fusion.5), channel_id=1, source_target_pairs={{0,6},{1,7},{2,0},{3,1},{4,2},{5,3},{6,4},{7,5},{8,14},{9,15},{10,... | collective-permute-start | bytes 3145736 | tf_op jit(solution)/shard_map/ppermute | solution.py:26
  232.8 26.5 %collective-permute-start.16 = (bf16[2,1,128,2048]{3,2,1,0:T(8,128)(2,1)S(1)}, bf16[2,1,128,2048]{3,2,1,0:T(8,128)(2,1)S(1)}, u32[]{:S(2)}, u32[]{:S(2)}) collective-permute-start(bf16[2,1,128,2048]{3,2,1,0:T(8,128)(2,1)S(1)} %constant_dynamic-update-slice_fusion.5), channel_id=1, source_target_pairs={{0,1},{1,0},{2,3},{3,2},{4,5},{5,4},{6,7},{7,6},{8,9},{9,8},{10,11... | collective-permute-start | bytes 3145736 | tf_op jit(solution)/shard_map/ppermute | solution.py:26
  255.9 16.1 %collective-permute-start.19 = (bf16[1,1,128,2048]{3,2,1,0:T(8,128)(2,1)S(1)}, bf16[1,1,128,2048]{3,2,1,0:T(8,128)(2,1)S(1)}, u32[]{:S(2)}, u32[]{:S(2)}) collective-permute-start(bf16[1,1,128,2048]{3,2,1,0:T(8,128)(2,1)S(1)} %slice.166), channel_id=1, source_target_pairs={{0,2},{1,3},{2,4},{3,5},{4,6},{5,7},{6,0},{7,1},{8,10},{9,11},{10,... | collective-permute-start | bytes 1572872 | tf_op jit(solution)/shard_map/ppermute | solution.py:26
  256.1 16.0 %collective-permute-start.20 = (bf16[1,1,128,2048]{3,2,1,0:T(8,128)(2,1)S(1)}, bf16[1,1,128,2048]{3,2,1,0:T(8,128)(2,1)S(1)}, u32[]{:S(2)}, u32[]{:S(2)}) collective-permute-start(bf16[1,1,128,2048]{3,2,1,0:T(8,128)(2,1)S(1)} %slice.167), channel_id=1, source_target_pairs={{0,6},{1,7},{2,0},{3,1},{4,2},{5,3},{6,4},{7,5},{8,14},{9,15},{10,... | collective-permute-start | bytes 1572872 | tf_op jit(solution)/shard_map/ppermute | solution.py:26
  259.4 33.3 %collective-permute-start.21 = (bf16[2,1,128,2048]{3,2,1,0:T(8,128)(2,1)S(1)}, bf16[2,1,128,2048]{3,2,1,0:T(8,128)(2,1)S(1)}, u32[]{:S(2)}, u32[]{:S(2)}) collective-permute-start(bf16[2,1,128,2048]{3,2,1,0:T(8,128)(2,1)S(1)} %collective-permute-done.16), channel_id=1, source_target_pairs={{0,2},{1,3},{2,4},{3,5},{4,6},{5,7},{6,0},{7,1},{8,10},{9,11},{10,... | collective-permute-start | bytes 3145736 | tf_op jit(solution)/shard_map/ppermute | solution.py:26
  259.4 33.3 %collective-permute-start.22 = (bf16[2,1,128,2048]{3,2,1,0:T(8,128)(2,1)S(1)}, bf16[2,1,128,2048]{3,2,1,0:T(8,128)(2,1)S(1)}, u32[]{:S(2)}, u32[]{:S(2)}) collective-permute-start(bf16[2,1,128,2048]{3,2,1,0:T(8,128)(2,1)S(1)} %collective-permute-done.16), channel_id=1, source_target_pairs={{0,6},{1,7},{2,0},{3,1},{4,2},{5,3},{6,4},{7,5},{8,14},{9,15},{10,... | collective-permute-start | bytes 3145736 | tf_op jit(solution)/shard_map/ppermute | solution.py:26
  272.2 21.6 %collective-permute-start.23 = (bf16[2,1,128,2048]{3,2,1,0:T(8,128)(2,1)S(1)}, bf16[2,1,128,2048]{3,2,1,0:T(8,128)(2,1)S(1)}, u32[]{:S(2)}, u32[]{:S(2)}) collective-permute-start(bf16[2,1,128,2048]{3,2,1,0:T(8,128)(2,1)S(1)} %constant_dynamic-update-slice_fusion.7), channel_id=1, source_target_pairs={{0,1},{1,0},{2,3},{3,2},{4,5},{5,4},{6,7},{7,6},{8,9},{9,8},{10,11... | collective-permute-start | bytes 3145736 | tf_op jit(solution)/shard_map/ppermute | solution.py:26
  273.5 1.1 copy-start.11
  273.5 1.3 copy-start.13
  295.7 1.1 copy-start.7
  295.8 1.3 copy-start.9
  298.2 1.8 copy-start.5
  299.9 1.2 copy-start.20
  299.9 1.4 copy-start.22
  299.9 1.5 copy-start.27
  301.4 2.5 copy-start.1
  (5 other events, 5.1 us)
